TPU v7x, 512 devices: a whole 4x8x8 slice. The times are simulated.
512 devices in a mesh: gx: 64 (over z, x, core), vert: 8 (over y).
Axes of the slice: x: 4, y: 8, z: 8, core: 2. Of those that a mesh axis runs over, the one named last changes fastest.
Arguments:
- position_factor: float32 [64, 8, 16, 256], P('gx'), may hold values from -6 to 6
- coefficients: float32 [256, 256], replicated, may hold values from -1 to 3
- velocity_factor: float32 [8, 64, 128, 256], P('vert', 'gx'), may hold values from -6 to 6
- gravity: float32 [3, 64, 8, 16], P(None, 'gx'), may hold values from -6 to 6
Outputs:
- new_position: float32 [64, 8, 16, 256], P('gx')
- new_velocity: float32 [8, 64, 128, 256], P('vert', 'gx')
All inputs are finite; a program needn't handle non-finite values.
Results may differ from a plain program's by a relative error of at most 0.0001.
Values sent between devices are 32-bit elements; how exact they have to be, the bound alone decides.
No kernel may reach another device: no remote copies, remote signals or barrier semaphores. Data moves between devices by JAX's collectives and lax.ppermute only.
A program may use at most 64 MiB of HBM per device.

v0:
```python
import jax
import jax.numpy as jnp
from jax import lax
from jax.sharding import Mesh
from jax.sharding import PartitionSpec as P

NS_STEPS = 8
GX = ("gx_0", "gx_1", "gx_2")


HIGHEST = lax.Precision.HIGHEST
TIME_STEP = 0.25
NORM_EPSILON = 1e-06


def padded_2(block, sides, width):
    for axis, dim in sides:
        count = lax.axis_size(axis)
        forward = [(i, i + 1) for i in range(count - 1)]
        backward = [(target, source) for source, target in forward]
        low = lax.ppermute(
            lax.slice_in_dim(block, block.shape[dim] - width, None, axis=dim), axis, forward
        )
        high = lax.ppermute(lax.slice_in_dim(block, 0, width, axis=dim), axis, backward)
        block = jnp.concatenate([low, block, high], axis=dim)
    return block


def extended(value, sides, width):
    edges = {}
    for axis, dim in sides:
        devices, length = (lax.axis_size(axis), value.shape[dim])
        up = [(i, (i + 1) % devices) for i in range(devices - 1)]
        last = lax.slice_in_dim(value, length - width, length, axis=dim)
        first = lax.slice_in_dim(value, 0, width, axis=dim)
        edges[dim] = (
            lax.ppermute(last, axis, up),
            lax.ppermute(first, axis, [(b, a) for a, b in up]),
        )
    done = []
    for _, dim in sides:
        low, high = edges[dim]
        around = [(width, width) if d in done else (0, 0) for d in range(value.ndim)]
        value = jnp.concatenate([jnp.pad(low, around), value, jnp.pad(high, around)], axis=dim)
        done.append(dim)
    return value


def from_behind(block, axis, distance):
    devices = range(lax.axis_size(axis))
    route = [(i - distance, i) for i in devices if i - distance in devices]
    return lax.ppermute(block, axis, route)


def filled_up(lines, devices):
    spare = -len(lines) % devices
    return jnp.pad(lines, [(0, spare)] + [(0, 0)] * (lines.ndim - 1))


def from_everyone(value, axis):
    devices = lax.axis_size(axis)
    return lax.all_to_all(
        jnp.broadcast_to(value[None], (devices, *value.shape)), axis, 0, 0, tiled=True
    )


def laid_out(pieces, dim):
    dims = list(pieces.shape[1:])
    dims[dim] *= pieces.shape[0]
    return jnp.moveaxis(pieces, 0, dim).reshape(dims)


def whole_of(value, axes, dim):
    far, near = axes
    pieces = from_everyone(from_everyone(value, far), near)
    return laid_out(pieces.swapaxes(0, 1).reshape(-1, *value.shape), dim)


def split_up(value, dim, devices):
    dims = value.shape
    pieces = value.reshape(*dims[:dim], devices, dims[dim] // devices, *dims[dim + 1 :])
    return jnp.moveaxis(pieces, dim, 0)


def sum_at_owner(value, axis, dim):
    devices = lax.axis_size(axis)
    pieces = lax.all_to_all(split_up(value, dim, devices), axis, 0, 0, tiled=True)
    return jnp.sum(pieces, axis=0)


def sum_in_two_steps(value, axes, dim):
    far, near = axes
    own = sum_at_owner(split_up(value, dim, lax.axis_size(far)), near, dim + 1)
    return jnp.sum(lax.all_to_all(own, far, 0, 0, tiled=True), axis=0)


def total_of(value, axes):
    lines = value.reshape(-1, value.shape[-1])
    padded = filled_up(lines, lax.axis_size(axes[0]) * lax.axis_size(axes[1]))
    whole = whole_of(sum_in_two_steps(padded, axes, 0), axes, 0)
    return lax.slice_in_dim(whole, 0, len(lines)).reshape(value.shape)


def total_of_2(value, axes):
    own = sum_in_two_steps(
        filled_up(value, lax.axis_size(axes[0]) * lax.axis_size(axes[1])), axes, 0
    )
    whole = whole_of(own, axes, 0)
    return whole[: len(value)].reshape(value.shape)


def in_one(arrays, axis):
    flat, at, done = (jnp.concatenate([a.reshape(-1) for a in arrays]), 0, [])
    running = total_of_2(flat, axis)
    for a in arrays:
        done.append(running[at : at + a.size].reshape(a.shape))
        at += a.size
    return tuple(done)


def staged_total(flat, axes):
    sizes = [lax.axis_size(a) for a in axes]
    devices = 1
    for n in sizes:
        devices *= n
    length = flat.shape[0]
    piece = -(-length // (devices * 128)) * 128
    part = jnp.pad(flat, (0, piece * devices - length))
    for axis, n in zip(axes, sizes):
        rows = part.reshape(n, -1, 128)
        part = jnp.sum(lax.all_to_all(rows, axis, 0, 0, tiled=True), axis=0).reshape(-1)
    for axis, n in zip(axes[::-1], sizes[::-1]):
        rows = jnp.broadcast_to(part.reshape(1, -1, 128), (n, part.shape[0] // 128, 128))
        part = lax.all_to_all(rows, axis, 0, 0, tiled=True).reshape(-1)
    return part[:length]


def split_parts(packed):
    flipped = jnp.swapaxes(packed, 1, 2)
    return jnp.stack([0.5 * (packed + flipped), 0.5 * (packed - flipped)])


def central(values, which_dim):
    padding = [(0, 0)] * values.ndim
    padding[which_dim] = (1, 1)
    padded = jnp.pad(values, padding)
    extent = values.shape[which_dim]
    return 0.5 * (
        lax.slice_in_dim(padded, 2, extent + 2, axis=which_dim)
        - lax.slice_in_dim(padded, 0, extent, axis=which_dim)
    )


def position_slopes(values):
    padded = padded_2(values, ((GX, 0),), 1)
    along_first = 0.5 * (padded[2:] - padded[:-2])
    return jnp.stack([along_first, central(values, 1), central(values, 2)])


def velocity_slopes(values):
    padded = extended(values, ((GX, 1), ("vert", 0)), 1)
    along_first = 0.5 * (padded[2:, 1:-1] - padded[:-2, 1:-1])
    along_second = 0.5 * (padded[1:-1, 2:] - padded[1:-1, :-2])
    return jnp.stack([along_first, along_second, central(values, 2)])


def coordinate(indices, cell_total):
    return (2.0 * indices.astype(jnp.float32) + 1.0 - cell_total) / cell_total


def velocity_grid(
    offset, slab_cells, first_count, second_offset, second_cells, second_count, third_count
):
    grid_shape = (slab_cells, second_cells, third_count)
    first_axis = coordinate(offset + jnp.arange(slab_cells, dtype=jnp.int32), first_count)
    second_axis = coordinate(
        second_offset + jnp.arange(second_cells, dtype=jnp.int32), second_count
    )
    third_axis = coordinate(jnp.arange(third_count, dtype=jnp.int32), third_count)
    return jnp.stack(
        [
            jnp.broadcast_to(first_axis[:, None, None], grid_shape),
            jnp.broadcast_to(second_axis[None, :, None], grid_shape),
            third_axis[None, None, :],
        ]
    )


def moments(factor, others, cells_count):
    return jnp.einsum("xyzr,dxyzs->drs", factor, others, precision=HIGHEST) / cells_count


def apply_pair(first_terms, first_mats, second_terms, second_mats):
    return -(
        jnp.einsum("dxyzs,drs->xyzr", first_terms, first_mats, precision=HIGHEST)
        + jnp.einsum("dxyzs,drs->xyzr", second_terms, second_mats, precision=HIGHEST)
    )


def newton_schulz(gram_matrix):
    frob_norm = jnp.sqrt(jnp.sum(gram_matrix * gram_matrix) + NORM_EPSILON)
    identity = jnp.eye(gram_matrix.shape[0], dtype=jnp.float32)
    root_part = gram_matrix / frob_norm
    inv_root = identity
    for sweep_index in range(NS_STEPS):
        middle = 1.5 * identity - 0.5 * jnp.dot(
            inv_root, root_part, precision=HIGHEST, preferred_element_type=jnp.float32
        )
        root_part = jnp.dot(
            root_part, middle, precision=HIGHEST, preferred_element_type=jnp.float32
        )
        inv_root = jnp.dot(middle, inv_root, precision=HIGHEST, preferred_element_type=jnp.float32)
    scale_root = jnp.sqrt(frob_norm)
    return (inv_root / scale_root, root_part * scale_root)


def sandwich(left_mats, core_matrix, right_mats):
    return jnp.einsum("dij,jk,dlk->il", left_mats, core_matrix, right_mats, precision=HIGHEST)


def per_device(position_factor, coefficients, velocity_factor, gravity):
    slab_vel = velocity_factor.shape[0]
    column_vel = velocity_factor.shape[1]
    first_count = slab_vel * lax.axis_size("vert")
    second_count = column_vel * lax.axis_size(GX)
    pos_cells = (
        position_factor.shape[0]
        * lax.axis_size(GX)
        * position_factor.shape[1]
        * position_factor.shape[2]
    )
    vel_cells = first_count * second_count * velocity_factor.shape[2]
    offset = lax.axis_index("vert") * slab_vel
    second_offset = lax.axis_index(GX) * column_vel
    velocity = velocity_grid(
        offset,
        slab_vel,
        first_count,
        second_offset,
        column_vel,
        second_count,
        velocity_factor.shape[2],
    )
    vel_first = moments(velocity_factor, velocity[..., None] * velocity_factor[None], vel_cells)
    next_plane = from_behind(velocity_factor, "vert", -1)
    next_column = from_behind(velocity_factor, GX, -1)
    following = jnp.concatenate([velocity_factor[1:], next_plane], axis=0)
    beside = jnp.concatenate([velocity_factor[:, 1:], next_column], axis=1)
    pair_sums = jnp.stack(
        [
            jnp.einsum("xyzr,xyzs->rs", velocity_factor, following, precision=HIGHEST),
            jnp.einsum("xyzr,xyzs->rs", velocity_factor, beside, precision=HIGHEST),
            jnp.einsum(
                "xyzr,xyzs->rs",
                velocity_factor[:, :, :-1],
                velocity_factor[:, :, 1:],
                precision=HIGHEST,
            ),
        ]
    )
    vel_second = 0.5 * (pair_sums - jnp.swapaxes(pair_sums, 1, 2)) / vel_cells
    vel_packed = (vel_first + vel_second).reshape(-1)
    vel_mats = split_parts(
        staged_total(vel_packed, ("gx_2", "gx_1", "vert", "gx_0")).reshape(vel_first.shape)
    )

    def position_rate(values):
        return apply_pair(
            position_slopes(values), vel_mats[0], gravity[..., None] * values[None], vel_mats[1]
        )

    initial = jnp.einsum("xyzs,sr->xyzr", position_factor, coefficients, precision=HIGHEST)
    section_one = initial + TIME_STEP * position_rate(initial)
    section_two = 0.75 * initial + 0.25 * (section_one + TIME_STEP * position_rate(section_one))
    final_section = 1.0 / 3.0 * initial + 2.0 / 3.0 * (
        section_two + TIME_STEP * position_rate(section_two)
    )
    gram_part = (
        jnp.einsum("xyzr,xyzs->rs", final_section, final_section, precision=HIGHEST) / pos_cells
    )
    raw_terms = jnp.stack(
        [
            moments(final_section, position_slopes(final_section), pos_cells),
            moments(final_section, gravity[..., None] * final_section[None], pos_cells),
        ]
    )
    local_packed = jnp.concatenate([gram_part[None], raw_terms[0] + raw_terms[1]])
    packed = staged_total(local_packed.reshape(-1), ("gx_2", "gx_1", "gx_0")).reshape(
        local_packed.shape
    )
    gram_matrix = 0.5 * (packed[0] + packed[0].T)
    second_raw, first_raw = split_parts(packed[1:])
    summed_terms = jnp.stack([first_raw, second_raw])
    inv_root, root_part = newton_schulz(gram_matrix)
    new_position = jnp.einsum("xyzs,sr->xyzr", final_section, inv_root, precision=HIGHEST)
    pos_mats = jnp.einsum("ir,ndij,js->ndrs", inv_root, summed_terms, inv_root, precision=HIGHEST)
    coupled_core = root_part + TIME_STEP * (
        sandwich(pos_mats[0], root_part, vel_mats[0])
        + sandwich(pos_mats[1], root_part, vel_mats[1])
    )

    def velocity_rate(values):
        return apply_pair(
            velocity[..., None] * values[None], pos_mats[0], velocity_slopes(values), pos_mats[1]
        )

    vel_initial = jnp.einsum("abcs,rs->abcr", velocity_factor, coupled_core, precision=HIGHEST)
    vel_section = vel_initial + TIME_STEP * velocity_rate(vel_initial)
    new_velocity = 0.5 * vel_initial + 0.5 * (vel_section + TIME_STEP * velocity_rate(vel_section))
    return (new_position, new_velocity)


def solution(mesh):
    finer = Mesh(
        mesh.devices.reshape(8, 4, 2, mesh.shape["vert"]), ("gx_0", "gx_1", "gx_2", "vert")
    )
    in_specs = (P(GX, None, None, None), P(), P("vert", GX, None, None), P(None, GX, None, None))
    out_specs = (P(GX, None, None, None), P("vert", GX, None, None))
    return jax.shard_map(
        per_device, mesh=finer, in_specs=in_specs, out_specs=out_specs, check_vma=False
    )
```

profile of v0, /device:TPU:80, one launch (start us, length us, event | category | flops | bytes accessed | tf_op | source)
XLA Modules:
  0.0 272.6 jit_solution(443016474092283801)
XLA Ops:
  14.5 4.4 %all_to_all.70 = f32[2,768,128]{2,1,0:T(8,128)S(1)} all-to-all(f32[2,768,128]{2,1,0:T(8,128)S(1)} %reshape.200), channel_id=1, replica_groups=mesh['gx_0'=8,'gx_1'=4,'gx_2'=2,'vert'=8] {'gx_2'}, dimensions={0} | all-to-all | bytes 1572864 | tf_op jit(solution)/shard_map/all_to_all | solution.py:131
  18.9 12.1 %all_to_all.71 = f32[4,192,128]{2,1,0:T(8,128)S(1)} all-to-all(f32[4,192,128]{2,1,0:T(8,128)S(1)} %bitcast.402), channel_id=1, replica_groups=mesh['gx_0'=8,'gx_1'=4,'gx_2'=2,'vert'=8] {'gx_1'}, dimensions={0} | all-to-all | bytes 786432 | tf_op jit(solution)/shard_map/all_to_all | solution.py:131
  31.1 13.5 %all_to_all.72 = f32[8,24,128]{2,1,0:T(8,128)S(1)} all-to-all(f32[8,24,128]{2,1,0:T(8,128)S(1)} %bitcast.413), channel_id=1, replica_groups=mesh['gx_0'=8,'gx_1'=4,'gx_2'=2,'vert'=8] {'vert'}, dimensions={0} | all-to-all | bytes 196608 | tf_op jit(solution)/shard_map/all_to_all | solution.py:131
  44.6 16.1 %all_to_all.73 = f32[8,3,128]{2,1,0:T(4,128)S(1)} all-to-all(f32[8,3,128]{2,1,0:T(4,128)S(1)} %reshape_reshape.30), channel_id=1, replica_groups=mesh['gx_0'=8,'gx_1'=4,'gx_2'=2,'vert'=8] {'gx_0'}, dimensions={0} | all-to-all | bytes 24576 | tf_op jit(solution)/shard_map/all_to_all | solution.py:131
  60.7 10.1 %all_to_all.74 = f32[8,3,128]{2,1,0:T(4,128)S(1)} all-to-all(f32[8,3,128]{2,1,0:T(4,128)S(1)} %broadcast_in_dim.26), channel_id=1, replica_groups=mesh['gx_0'=8,'gx_1'=4,'gx_2'=2,'vert'=8] {'gx_0'}, dimensions={0} | all-to-all | bytes 24576 | tf_op jit(solution)/shard_map/all_to_all | solution.py:134
  71.5 5.8 %all-to-all-start.5 = ((f32[8,24,128]{2,1,0:T(8,128)}), f32[8,24,128]{2,1,0:T(8,128)S(1)}, u32[]{:S(2)}, u32[]{:S(2)}) async-start(f32[8,24,128]{2,1,0:T(8,128)} %broadcast_in_dim.28), calls=%async_computation.5 | async-start | bytes 196608 | tf_op jit(solution)/shard_map/all_to_all | solution.py:134
  79.5 5.8 %collective-permute-start = (f32[1,8,16,256]{3,2,1,0:T(8,128)S(1)}, f32[1,8,16,256]{3,2,1,0:T(8,128)S(1)}, u32[]{:S(2)}, u32[]{:S(2)}) collective-permute-start(f32[1,8,16,256]{3,2,1,0:T(8,128)S(1)} %bitcast.385), channel_id=1, source_target_pairs={{8,0},{16,8},{24,16},{32,24},{40,32},{48,40},{56,48},{64,56},{72,6... | collective-permute-start | bytes 393224 | tf_op jit(solution)/shard_map/ppermute | solution.py:24
  86.1 3.5 %all-to-all-start.6 = ((f32[4,192,128]{2,1,0:T(8,128)}), f32[4,192,128]{2,1,0:T(8,128)S(1)}, u32[]{:S(2)}, u32[]{:S(2)}) async-start(f32[4,192,128]{2,1,0:T(8,128)} %broadcast_in_dim.30), calls=%async_computation.6 | async-start | bytes 786432 | tf_op jit(solution)/shard_map/all_to_all | solution.py:134
  89.6 7.2 %all-to-all-done.6 = f32[4,192,128]{2,1,0:T(8,128)S(1)} async-done(((f32[4,192,128]{2,1,0:T(8,128)}), f32[4,192,128]{2,1,0:T(8,128)S(1)}, u32[]{:S(2)}, u32[]{:S(2)}) %all-to-all-start.6) | async-done | bytes 393248 | tf_op jit(solution)/shard_map/all_to_all | solution.py:134
  96.9 4.4 %all_to_all.75 = f32[2,768,128]{2,1,0:T(8,128)S(1)} all-to-all(f32[2,768,128]{2,1,0:T(8,128)S(1)} %broadcast_in_dim.32), channel_id=1, replica_groups=mesh['gx_0'=8,'gx_1'=4,'gx_2'=2,'vert'=8] {'gx_2'}, dimensions={0} | all-to-all | bytes 1572864 | tf_op jit(solution)/shard_map/all_to_all | solution.py:134
  107.1 5.6 %collective-permute-start.4 = (f32[1,8,16,256]{3,2,1,0:T(8,128)S(1)}, f32[1,8,16,256]{3,2,1,0:T(8,128)S(1)}, u32[]{:S(2)}, u32[]{:S(2)}) collective-permute-start(f32[1,8,16,256]{3,2,1,0:T(8,128)S(1)} %bitcast.396), channel_id=1, source_target_pairs={{8,0},{16,8},{24,16},{32,24},{40,32},{48,40},{56,48},{64,56},{72,6... | collective-permute-start | bytes 393224 | tf_op jit(solution)/shard_map/ppermute | solution.py:24
  117.7 5.9 %collective-permute-start.6 = (f32[1,8,16,256]{3,2,1,0:T(8,128)S(1)}, f32[1,8,16,256]{3,2,1,0:T(8,128)S(1)}, u32[]{:S(2)}, u32[]{:S(2)}) collective-permute-start(f32[1,8,16,256]{3,2,1,0:T(8,128)S(1)} %bitcast.399), channel_id=1, source_target_pairs={{8,0},{16,8},{24,16},{32,24},{40,32},{48,40},{56,48},{64,56},{72,6... | collective-permute-start | bytes 393224 | tf_op jit(solution)/shard_map/ppermute | solution.py:24
  128.6 5.9 %collective-permute-start.8 = (f32[1,8,16,256]{3,2,1,0:T(8,128)S(1)}, f32[1,8,16,256]{3,2,1,0:T(8,128)S(1)}, u32[]{:S(2)}, u32[]{:S(2)}) collective-permute-start(f32[1,8,16,256]{3,2,1,0:T(8,128)S(1)} %bitcast.409), channel_id=1, source_target_pairs={{8,0},{16,8},{24,16},{32,24},{40,32},{48,40},{56,48},{64,56},{72,6... | collective-permute-start | bytes 393224 | tf_op jit(solution)/shard_map/ppermute | solution.py:24
  141.7 5.4 %all_to_all.76 = f32[2,1024,128]{2,1,0:T(8,128)} all-to-all(f32[2,1024,128]{2,1,0:T(8,128)S(1)} %reshape.204), channel_id=1, replica_groups=mesh['gx_0'=8,'gx_1'=4,'gx_2'=2,'vert'=8] {'gx_2'}, dimensions={0} | all-to-all | bytes 2097152 | tf_op jit(solution)/shard_map/all_to_all | solution.py:131
  148.4 13.8 %all_to_all.77 = f32[4,256,128]{2,1,0:T(8,128)S(1)} all-to-all(f32[4,256,128]{2,1,0:T(8,128)S(1)} %bitcast.394), channel_id=1, replica_groups=mesh['gx_0'=8,'gx_1'=4,'gx_2'=2,'vert'=8] {'gx_1'}, dimensions={0} | all-to-all | bytes 1048576 | tf_op jit(solution)/shard_map/all_to_all | solution.py:131
  162.2 15.6 %all_to_all.78 = f32[8,32,128]{2,1,0:T(8,128)S(1)} all-to-all(f32[8,32,128]{2,1,0:T(8,128)S(1)} %bitcast.412), channel_id=1, replica_groups=mesh['gx_0'=8,'gx_1'=4,'gx_2'=2,'vert'=8] {'gx_0'}, dimensions={0} | all-to-all | bytes 262144 | tf_op jit(solution)/shard_map/all_to_all | solution.py:131
  177.9 11.5 %all_to_all.79 = f32[8,32,128]{2,1,0:T(8,128)S(1)} all-to-all(f32[8,32,128]{2,1,0:T(8,128)S(1)} %broadcast_in_dim.34), channel_id=1, replica_groups=mesh['gx_0'=8,'gx_1'=4,'gx_2'=2,'vert'=8] {'gx_0'}, dimensions={0} | all-to-all | bytes 262144 | tf_op jit(solution)/shard_map/all_to_all | solution.py:134
  189.4 10.5 %all_to_all.80 = f32[4,256,128]{2,1,0:T(8,128)S(1)} all-to-all(f32[4,256,128]{2,1,0:T(8,128)S(1)} %broadcast_in_dim.36), channel_id=1, replica_groups=mesh['gx_0'=8,'gx_1'=4,'gx_2'=2,'vert'=8] {'gx_1'}, dimensions={0} | all-to-all | bytes 1048576 | tf_op jit(solution)/shard_map/all_to_all | solution.py:134
  199.9 5.4 %all_to_all.81 = f32[2,1024,128]{2,1,0:T(8,128)} all-to-all(f32[2,1024,128]{2,1,0:T(8,128)S(1)} %broadcast_in_dim.76), channel_id=1, replica_groups=mesh['gx_0'=8,'gx_1'=4,'gx_2'=2,'vert'=8] {'gx_2'}, dimensions={0} | all-to-all | bytes 2097152 | tf_op jit(solution)/shard_map/all_to_all | solution.py:134
  231.0 5.6 %collective-permute-start.12 = (f32[1,1,128,256]{3,2,1,0:T(8,128)S(1)}, f32[1,1,128,256]{3,2,1,0:T(8,128)S(1)}, u32[]{:S(2)}, u32[]{:S(2)}) collective-permute-start(f32[1,1,128,256]{3,2,1,0:T(8,128)S(1)} %bitcast.389), channel_id=1, source_target_pairs={{8,0},{16,8},{24,16},{32,24},{40,32},{48,40},{56,48},{64,56},{72,6... | collective-permute-start | bytes 393224 | tf_op jit(solution)/shard_map/ppermute | solution.py:38
  243.5 4.0 %collective-permute-done.10 = f32[1,1,128,256]{3,2,1,0:T(8,128)S(1)} collective-permute-done((f32[1,1,128,256]{3,2,1,0:T(8,128)S(1)}, f32[1,1,128,256]{3,2,1,0:T(8,128)S(1)}, u32[]{:S(2)}, u32[]{:S(2)}) %collective-permute-start.10) | collective-permute-done | bytes 131104 | tf_op jit(solution)/shard_map/ppermute | solution.py:38
  251.4 5.8 %collective-permute-start.16 = (f32[1,1,128,256]{3,2,1,0:T(8,128)S(1)}, f32[1,1,128,256]{3,2,1,0:T(8,128)S(1)}, u32[]{:S(2)}, u32[]{:S(2)}) collective-permute-start(f32[1,1,128,256]{3,2,1,0:T(8,128)S(1)} %bitcast.404), channel_id=1, source_target_pairs={{8,0},{16,8},{24,16},{32,24},{40,32},{48,40},{56,48},{64,56},{72,6... | collective-permute-start | bytes 393224 | tf_op jit(solution)/shard_map/ppermute | solution.py:38
  258.1 5.1 %collective-permute-start.15 = (f32[1,1,128,256]{3,2,1,0:T(8,128)S(1)}, f32[1,1,128,256]{3,2,1,0:T(8,128)S(1)}, u32[]{:S(2)}, u32[]{:S(2)}) collective-permute-start(f32[1,1,128,256]{3,2,1,0:T(8,128)S(1)} %bitcast.405), channel_id=1, source_target_pairs={{0,1},{1,2},{2,3},{3,4},{4,5},{5,6},{6,7},{8,9},{9,10},{10,11},{11... | collective-permute-start | bytes 393224 | tf_op jit(solution)/shard_map/ppermute | solution.py:37
  265.7 4.4 %collective-permute-done.14 = f32[1,1,128,256]{3,2,1,0:T(8,128)S(1)} collective-permute-done((f32[1,1,128,256]{3,2,1,0:T(8,128)S(1)}, f32[1,1,128,256]{3,2,1,0:T(8,128)S(1)}, u32[]{:S(2)}, u32[]{:S(2)}) %collective-permute-start.14) | collective-permute-done | bytes 131104 | tf_op jit(solution)/shard_map/ppermute | solution.py:38
  (141 shorter events, 83.2 us)
Async XLA Ops:
  0.6 76.7 %copy-start = (f32[256,256]{1,0:T(8,128)S(1)}, f32[256,256]{1,0:T(8,128)}, u32[]{:S(2)}) copy-start(f32[256,256]{1,0:T(8,128)} %param.5) | copy-start | bytes 786436
  0.6 7.3 %collective-permute-start.3 = (f32[1,1,128,256]{3,2,1,0:T(8,128)}, f32[1,1,128,256]{3,2,1,0:T(8,128)S(1)}, u32[]{:S(2)}, u32[]{:S(2)}) collective-permute-start(f32[1,1,128,256]{3,2,1,0:T(8,128)} %param.6), channel_id=1, source_target_pairs={{8,0},{16,8},{24,16},{32,24},{40,32},{48,40},{56,48},{64,56},{72,6... | collective-permute-start | bytes 393224 | tf_op jit(solution)/shard_map/ppermute | solution.py:52
  4.0 7.1 %collective-permute-start.2 = (f32[1,1,128,256]{3,2,1,0:T(8,128)}, f32[1,1,128,256]{3,2,1,0:T(8,128)S(1)}, u32[]{:S(2)}, u32[]{:S(2)}) collective-permute-start(f32[1,1,128,256]{3,2,1,0:T(8,128)} %param.6), channel_id=1, source_target_pairs={{1,0},{2,1},{3,2},{4,3},{5,4},{6,5},{7,6},{9,8},{10,9},{11,10},{12... | collective-permute-start | bytes 393224 | tf_op jit(solution)/shard_map/ppermute | solution.py:52
  18.9 58.4 %copy-start.4 = (f32[1,8,16,256]{3,2,1,0:T(8,128)S(1)}, f32[1,8,16,256]{3,2,1,0:T(8,128)}, u32[]{:S(2)}) copy-start(f32[1,8,16,256]{3,2,1,0:T(8,128)} %param.4) | copy-start | bytes 393220
  71.5 13.8 %all-to-all-start.5 = ((f32[8,24,128]{2,1,0:T(8,128)}), f32[8,24,128]{2,1,0:T(8,128)S(1)}, u32[]{:S(2)}, u32[]{:S(2)}) async-start(f32[8,24,128]{2,1,0:T(8,128)} %broadcast_in_dim.28), calls=%async_computation.5 | async-start | bytes 196608 | tf_op jit(solution)/shard_map/all_to_all | solution.py:134
  77.6 12.0 %collective-permute-start.1 = (f32[1,8,16,256]{3,2,1,0:T(8,128)S(1)}, f32[1,8,16,256]{3,2,1,0:T(8,128)S(1)}, u32[]{:S(2)}, u32[]{:S(2)}) collective-permute-start(f32[1,8,16,256]{3,2,1,0:T(8,128)S(1)} %bitcast.384), channel_id=1, source_target_pairs={{0,8},{8,16},{16,24},{24,32},{32,40},{40,48},{48,56},{56,64},{64,7... | collective-permute-start | bytes 393224 | tf_op jit(solution)/shard_map/ppermute | solution.py:21
  79.5 10.1 %collective-permute-start = (f32[1,8,16,256]{3,2,1,0:T(8,128)S(1)}, f32[1,8,16,256]{3,2,1,0:T(8,128)S(1)}, u32[]{:S(2)}, u32[]{:S(2)}) collective-permute-start(f32[1,8,16,256]{3,2,1,0:T(8,128)S(1)} %bitcast.385), channel_id=1, source_target_pairs={{8,0},{16,8},{24,16},{32,24},{40,32},{48,40},{56,48},{64,56},{72,6... | collective-permute-start | bytes 393224 | tf_op jit(solution)/shard_map/ppermute | solution.py:24
  86.1 10.8 %all-to-all-start.6 = ((f32[4,192,128]{2,1,0:T(8,128)}), f32[4,192,128]{2,1,0:T(8,128)S(1)}, u32[]{:S(2)}, u32[]{:S(2)}) async-start(f32[4,192,128]{2,1,0:T(8,128)} %broadcast_in_dim.30), calls=%async_computation.6 | async-start | bytes 786432 | tf_op jit(solution)/shard_map/all_to_all | solution.py:134
  105.1 8.4 %collective-permute-start.5 = (f32[1,8,16,256]{3,2,1,0:T(8,128)S(1)}, f32[1,8,16,256]{3,2,1,0:T(8,128)S(1)}, u32[]{:S(2)}, u32[]{:S(2)}) collective-permute-start(f32[1,8,16,256]{3,2,1,0:T(8,128)S(1)} %bitcast.395), channel_id=1, source_target_pairs={{0,8},{8,16},{16,24},{24,32},{32,40},{40,48},{48,56},{56,64},{64,7... | collective-permute-start | bytes 393224 | tf_op jit(solution)/shard_map/ppermute | solution.py:21
  107.1 8.1 %collective-permute-start.4 = (f32[1,8,16,256]{3,2,1,0:T(8,128)S(1)}, f32[1,8,16,256]{3,2,1,0:T(8,128)S(1)}, u32[]{:S(2)}, u32[]{:S(2)}) collective-permute-start(f32[1,8,16,256]{3,2,1,0:T(8,128)S(1)} %bitcast.396), channel_id=1, source_target_pairs={{8,0},{16,8},{24,16},{32,24},{40,32},{48,40},{56,48},{64,56},{72,6... | collective-permute-start | bytes 393224 | tf_op jit(solution)/shard_map/ppermute | solution.py:24
  115.8 8.5 %collective-permute-start.7 = (f32[1,8,16,256]{3,2,1,0:T(8,128)S(1)}, f32[1,8,16,256]{3,2,1,0:T(8,128)S(1)}, u32[]{:S(2)}, u32[]{:S(2)}) collective-permute-start(f32[1,8,16,256]{3,2,1,0:T(8,128)S(1)} %bitcast.398), channel_id=1, source_target_pairs={{0,8},{8,16},{16,24},{24,32},{32,40},{40,48},{48,56},{56,64},{64,7... | collective-permute-start | bytes 393224 | tf_op jit(solution)/shard_map/ppermute | solution.py:21
  117.7 8.4 %collective-permute-start.6 = (f32[1,8,16,256]{3,2,1,0:T(8,128)S(1)}, f32[1,8,16,256]{3,2,1,0:T(8,128)S(1)}, u32[]{:S(2)}, u32[]{:S(2)}) collective-permute-start(f32[1,8,16,256]{3,2,1,0:T(8,128)S(1)} %bitcast.399), channel_id=1, source_target_pairs={{8,0},{16,8},{24,16},{32,24},{40,32},{48,40},{56,48},{64,56},{72,6... | collective-permute-start | bytes 393224 | tf_op jit(solution)/shard_map/ppermute | solution.py:24
  126.7 10.4 %copy-start.2 = (f32[8,16,256]{2,1,0:T(8,128)}, f32[8,16,256]{2,1,0:T(8,128)S(1)}, u32[]{:S(2)}) copy-start(f32[8,16,256]{2,1,0:T(8,128)S(1)} %fusion.37) | copy-start | bytes 393220
  126.7 10.2 %collective-permute-start.9 = (f32[1,8,16,256]{3,2,1,0:T(8,128)S(1)}, f32[1,8,16,256]{3,2,1,0:T(8,128)S(1)}, u32[]{:S(2)}, u32[]{:S(2)}) collective-permute-start(f32[1,8,16,256]{3,2,1,0:T(8,128)S(1)} %bitcast.408), channel_id=1, source_target_pairs={{0,8},{8,16},{16,24},{24,32},{32,40},{40,48},{48,56},{56,64},{64,7... | collective-permute-start | bytes 393224 | tf_op jit(solution)/shard_map/ppermute | solution.py:21
  128.6 8.4 %collective-permute-start.8 = (f32[1,8,16,256]{3,2,1,0:T(8,128)S(1)}, f32[1,8,16,256]{3,2,1,0:T(8,128)S(1)}, u32[]{:S(2)}, u32[]{:S(2)}) collective-permute-start(f32[1,8,16,256]{3,2,1,0:T(8,128)S(1)} %bitcast.409), channel_id=1, source_target_pairs={{8,0},{16,8},{24,16},{32,24},{40,32},{48,40},{56,48},{64,56},{72,6... | collective-permute-start | bytes 393224 | tf_op jit(solution)/shard_map/ppermute | solution.py:24
  229.0 13.6 %collective-permute-start.13 = (f32[1,1,128,256]{3,2,1,0:T(8,128)S(1)}, f32[1,1,128,256]{3,2,1,0:T(8,128)S(1)}, u32[]{:S(2)}, u32[]{:S(2)}) collective-permute-start(f32[1,1,128,256]{3,2,1,0:T(8,128)S(1)} %bitcast.388), channel_id=1, source_target_pairs={{0,8},{8,16},{16,24},{24,32},{32,40},{40,48},{48,56},{56,64},{64,7... | collective-permute-start | bytes 393224 | tf_op jit(solution)/shard_map/ppermute | solution.py:37
  231.0 11.6 %collective-permute-start.12 = (f32[1,1,128,256]{3,2,1,0:T(8,128)S(1)}, f32[1,1,128,256]{3,2,1,0:T(8,128)S(1)}, u32[]{:S(2)}, u32[]{:S(2)}) collective-permute-start(f32[1,1,128,256]{3,2,1,0:T(8,128)S(1)} %bitcast.389), channel_id=1, source_target_pairs={{8,0},{16,8},{24,16},{32,24},{40,32},{48,40},{56,48},{64,56},{72,6... | collective-permute-start | bytes 393224 | tf_op jit(solution)/shard_map/ppermute | solution.py:38
  236.7 6.9 %collective-permute-start.11 = (f32[1,1,128,256]{3,2,1,0:T(8,128)S(1)}, f32[1,1,128,256]{3,2,1,0:T(8,128)S(1)}, u32[]{:S(2)}, u32[]{:S(2)}) collective-permute-start(f32[1,1,128,256]{3,2,1,0:T(8,128)S(1)} %bitcast.390), channel_id=1, source_target_pairs={{0,1},{1,2},{2,3},{3,4},{4,5},{5,6},{6,7},{8,9},{9,10},{10,11},{11... | collective-permute-start | bytes 393224 | tf_op jit(solution)/shard_map/ppermute | solution.py:37
  240.0 7.5 %collective-permute-start.10 = (f32[1,1,128,256]{3,2,1,0:T(8,128)S(1)}, f32[1,1,128,256]{3,2,1,0:T(8,128)S(1)}, u32[]{:S(2)}, u32[]{:S(2)}) collective-permute-start(f32[1,1,128,256]{3,2,1,0:T(8,128)S(1)} %bitcast.391), channel_id=1, source_target_pairs={{1,0},{2,1},{3,2},{4,3},{5,4},{6,5},{7,6},{9,8},{10,9},{11,10},{12... | collective-permute-start | bytes 393224 | tf_op jit(solution)/shard_map/ppermute | solution.py:38
  242.6 14.6 %copy-start.3 = (f32[8,16,256]{2,1,0:T(8,128)S(1)}, f32[8,16,256]{2,1,0:T(8,128)}, u32[]{:S(2)}) copy-start(f32[8,16,256]{2,1,0:T(8,128)} %copy-done.2) | copy-start | bytes 393220
  249.4 15.7 %collective-permute-start.17 = (f32[1,1,128,256]{3,2,1,0:T(8,128)S(1)}, f32[1,1,128,256]{3,2,1,0:T(8,128)S(1)}, u32[]{:S(2)}, u32[]{:S(2)}) collective-permute-start(f32[1,1,128,256]{3,2,1,0:T(8,128)S(1)} %bitcast.403), channel_id=1, source_target_pairs={{0,8},{8,16},{16,24},{24,32},{32,40},{40,48},{48,56},{56,64},{64,7... | collective-permute-start | bytes 393224 | tf_op jit(solution)/shard_map/ppermute | solution.py:37
  251.4 13.8 %collective-permute-start.16 = (f32[1,1,128,256]{3,2,1,0:T(8,128)S(1)}, f32[1,1,128,256]{3,2,1,0:T(8,128)S(1)}, u32[]{:S(2)}, u32[]{:S(2)}) collective-permute-start(f32[1,1,128,256]{3,2,1,0:T(8,128)S(1)} %bitcast.404), channel_id=1, source_target_pairs={{8,0},{16,8},{24,16},{32,24},{40,32},{48,40},{56,48},{64,56},{72,6... | collective-permute-start | bytes 393224 | tf_op jit(solution)/shard_map/ppermute | solution.py:38
  258.1 7.6 %collective-permute-start.15 = (f32[1,1,128,256]{3,2,1,0:T(8,128)S(1)}, f32[1,1,128,256]{3,2,1,0:T(8,128)S(1)}, u32[]{:S(2)}, u32[]{:S(2)}) collective-permute-start(f32[1,1,128,256]{3,2,1,0:T(8,128)S(1)} %bitcast.405), channel_id=1, source_target_pairs={{0,1},{1,2},{2,3},{3,4},{4,5},{5,6},{6,7},{8,9},{9,10},{10,11},{11... | collective-permute-start | bytes 393224 | tf_op jit(solution)/shard_map/ppermute | solution.py:37
  263.2 6.9 %collective-permute-start.14 = (f32[1,1,128,256]{3,2,1,0:T(8,128)S(1)}, f32[1,1,128,256]{3,2,1,0:T(8,128)S(1)}, u32[]{:S(2)}, u32[]{:S(2)}) collective-permute-start(f32[1,1,128,256]{3,2,1,0:T(8,128)S(1)} %bitcast.406), channel_id=1, source_target_pairs={{1,0},{2,1},{3,2},{4,3},{5,4},{6,5},{7,6},{9,8},{10,9},{11,10},{12... | collective-permute-start | bytes 393224 | tf_op jit(solution)/shard_map/ppermute | solution.py:38
  (2 other events, 2.2 us)
where the time goes:
time: 274 us; the launch traced here: 273 us
  blocking collectives  123 us (45%)
  starting transfers between devices  74.1 us (27%)
  matrix products  33.7 us (12%)
  waiting for transfers between devices  22.8 us (8%)
  local copies, waits for them, and re-layouts  11.8 us (4%)
  other arithmetic  5.34 us (2%)
    all_to_all x7, blocking collectives, staged_total(): lax.all_to_all(rows, axis, 0, 0, tiled=True)  80.8 us
    all_to_all x5, blocking collectives, staged_total(): part = lax.all_to_all(rows, axis, 0, 0, tiled=True).reshape(-1)  41.8 us
    ppermute x4, starting transfers between devices, padded_2(): lax.ppermute(lax.slice_in_dim(block, 0, width, axis=dim), axis, backward)  23.2 us
    ppermute x4, starting transfers between devices, extended(): lax.ppermute(first, axis, [(b, a) for a, b in up])  15.8 us
    ppermute x4, starting transfers between devices, extended(): lax.ppermute(last, axis, up)  12.5 us
    all_to_all x2, starting transfers between devices, staged_total(): part = lax.all_to_all(rows, axis, 0, 0, tiled=True).reshape(-1)  9.22 us
    ppermute x4, waiting for transfers between devices, extended(): lax.ppermute(first, axis, [(b, a) for a, b in up])  8.42 us
    ppermute x4, starting transfers between devices, padded_2(): lax.ppermute(lax.slice_in_dim(block, block.shape[dim] - width, None, axis...  7.81 us
  transfers between devices with their start and end apart: 20, of which 11 were waited for; matrix products, arithmetic and copies ran while one was open for 3% of the time, Pallas kernels for 0%

commit v1 on v0

--- a/solution.py
+++ b/solution.py
@@ -261,7 +261,7 @@
     vel_second = 0.5 * (pair_sums - jnp.swapaxes(pair_sums, 1, 2)) / vel_cells
     vel_packed = (vel_first + vel_second).reshape(-1)
     vel_mats = split_parts(
-        staged_total(vel_packed, ("gx_2", "gx_1", "vert", "gx_0")).reshape(vel_first.shape)
+        staged_total(vel_packed, (("gx_1", "gx_2"), "vert", "gx_0")).reshape(vel_first.shape)
     )
 
     def position_rate(values):
@@ -285,7 +285,7 @@
         ]
     )
     local_packed = jnp.concatenate([gram_part[None], raw_terms[0] + raw_terms[1]])
-    packed = staged_total(local_packed.reshape(-1), ("gx_2", "gx_1", "gx_0")).reshape(
+    packed = staged_total(local_packed.reshape(-1), (("gx_1", "gx_2"), "gx_0")).reshape(
         local_packed.shape
     )
     gram_matrix = 0.5 * (packed[0] + packed[0].T)

time: 274 us -> 274 us (level)
  the two profiles are of different devices: /device:TPU:80 before, /device:TPU:64 now
where the time goes in v1:
time: 274 us; the launch traced here: 272 us
  blocking collectives  135 us (49%)
  starting transfers between devices  61.9 us (23%)
  matrix products  33.7 us (12%)
  waiting for transfers between devices  23.8 us (9%)
  local copies, waits for them, and re-layouts  11.1 us (4%)
  other arithmetic  5.22 us (2%)
    all_to_all x5, blocking collectives, staged_total(): lax.all_to_all(rows, axis, 0, 0, tiled=True)  83.4 us
    all_to_all x4, blocking collectives, staged_total(): part = lax.all_to_all(rows, axis, 0, 0, tiled=True).reshape(-1)  51.1 us
    ppermute x4, starting transfers between devices, padded_2(): lax.ppermute(lax.slice_in_dim(block, 0, width, axis=dim), axis, backward)  22.9 us
    ppermute x4, starting transfers between devices, extended(): lax.ppermute(first, axis, [(b, a) for a, b in up])  14.1 us
    ppermute x4, waiting for transfers between devices, extended(): lax.ppermute(first, axis, [(b, a) for a, b in up])  8.73 us
    ppermute x4, starting transfers between devices, extended(): lax.ppermute(last, axis, up)  8.65 us
    ppermute x4, starting transfers between devices, padded_2(): lax.ppermute(lax.slice_in_dim(block, block.shape[dim] - width, None, axis...  8.06 us
    ppermute x4, waiting for transfers between devices, padded_2(): lax.ppermute(lax.slice_in_dim(block, 0, width, axis=dim), axis, backward)  5.7 us
  transfers between devices with their start and end apart: 19, of which 13 were waited for; matrix products, arithmetic and copies ran while one was open for 3% of the time, Pallas kernels for 0%

profile of v1, /device:TPU:64, one launch (start us, length us, event | category | flops | bytes accessed | tf_op | source)
XLA Modules:
  0.0 272.5 jit_solution(10499125007412993024)
XLA Ops:
  0.6 3.3 %collective-permute-start.3 = (f32[1,1,128,256]{3,2,1,0:T(8,128)}, f32[1,1,128,256]{3,2,1,0:T(8,128)S(1)}, u32[]{:S(2)}, u32[]{:S(2)}) collective-permute-start(f32[1,1,128,256]{3,2,1,0:T(8,128)} %param.6), channel_id=1, source_target_pairs={{8,0},{16,8},{24,16},{32,24},{40,32},{48,40},{56,48},{64,56},{72,6... | collective-permute-start | bytes 393224 | tf_op jit(solution)/shard_map/ppermute | solution.py:52
  8.2 2.9 %collective-permute-done.2 = f32[1,1,128,256]{3,2,1,0:T(8,128)S(1)} collective-permute-done((f32[1,1,128,256]{3,2,1,0:T(8,128)}, f32[1,1,128,256]{3,2,1,0:T(8,128)S(1)}, u32[]{:S(2)}, u32[]{:S(2)}) %collective-permute-start.2) | collective-permute-done | bytes 131104 | tf_op jit(solution)/shard_map/ppermute | solution.py:52
  14.5 16.9 %all_to_all.50 = f32[8,192,128]{2,1,0:T(8,128)S(1)} all-to-all(f32[8,192,128]{2,1,0:T(8,128)S(1)} %reshape.201), channel_id=1, replica_groups=mesh['gx_0'=8,'gx_1'=4,'gx_2'=2,'vert'=8] {'gx_1','gx_2'}, dimensions={0} | all-to-all | bytes 1572864 | tf_op jit(solution)/shard_map/all_to_all | solution.py:131
  31.5 15.8 %all_to_all.51 = f32[8,24,128]{2,1,0:T(8,128)S(1)} all-to-all(f32[8,24,128]{2,1,0:T(8,128)S(1)} %bitcast.393), channel_id=1, replica_groups=mesh['gx_0'=8,'gx_1'=4,'gx_2'=2,'vert'=8] {'vert'}, dimensions={0} | all-to-all | bytes 196608 | tf_op jit(solution)/shard_map/all_to_all | solution.py:131
  47.3 16.1 %all_to_all.52 = f32[8,3,128]{2,1,0:T(4,128)S(1)} all-to-all(f32[8,3,128]{2,1,0:T(4,128)S(1)} %reshape_reshape.9), channel_id=1, replica_groups=mesh['gx_0'=8,'gx_1'=4,'gx_2'=2,'vert'=8] {'gx_0'}, dimensions={0} | all-to-all | bytes 24576 | tf_op jit(solution)/shard_map/all_to_all | solution.py:131
  63.4 10.1 %all_to_all.53 = f32[8,3,128]{2,1,0:T(4,128)S(1)} all-to-all(f32[8,3,128]{2,1,0:T(4,128)S(1)} %broadcast_in_dim.18), channel_id=1, replica_groups=mesh['gx_0'=8,'gx_1'=4,'gx_2'=2,'vert'=8] {'gx_0'}, dimensions={0} | all-to-all | bytes 24576 | tf_op jit(solution)/shard_map/all_to_all | solution.py:134
  73.6 11.1 %all_to_all.54 = f32[8,24,128]{2,1,0:T(8,128)S(1)} all-to-all(f32[8,24,128]{2,1,0:T(8,128)S(1)} %broadcast_in_dim.20), channel_id=1, replica_groups=mesh['gx_0'=8,'gx_1'=4,'gx_2'=2,'vert'=8] {'vert'}, dimensions={0} | all-to-all | bytes 196608 | tf_op jit(solution)/shard_map/all_to_all | solution.py:134
  85.7 3.5 %all-to-all-start.5 = ((f32[8,192,128]{2,1,0:T(8,128)}), f32[8,192,128]{2,1,0:T(8,128)S(1)}, u32[]{:S(2)}, u32[]{:S(2)}) async-start(f32[8,192,128]{2,1,0:T(8,128)} %broadcast_in_dim.22), calls=%async_computation.5 | async-start | bytes 1572864 | tf_op jit(solution)/shard_map/all_to_all | solution.py:134
  89.5 2.3 collective-permute-start.1
  91.8 5.4 %collective-permute-start = (f32[1,8,16,256]{3,2,1,0:T(8,128)S(1)}, f32[1,8,16,256]{3,2,1,0:T(8,128)S(1)}, u32[]{:S(2)}, u32[]{:S(2)}) collective-permute-start(f32[1,8,16,256]{3,2,1,0:T(8,128)S(1)} %bitcast.369), channel_id=1, source_target_pairs={{8,0},{16,8},{24,16},{32,24},{40,32},{48,40},{56,48},{64,56},{72,6... | collective-permute-start | bytes 393224 | tf_op jit(solution)/shard_map/ppermute | solution.py:24
  100.1 3.3 %all-to-all-done.5 = f32[8,192,128]{2,1,0:T(8,128)S(1)} async-done(((f32[8,192,128]{2,1,0:T(8,128)}), f32[8,192,128]{2,1,0:T(8,128)S(1)}, u32[]{:S(2)}, u32[]{:S(2)}) %all-to-all-start.5) | async-done | bytes 786464 | tf_op jit(solution)/shard_map/all_to_all | solution.py:134
  109.1 5.8 %collective-permute-start.4 = (f32[1,8,16,256]{3,2,1,0:T(8,128)S(1)}, f32[1,8,16,256]{3,2,1,0:T(8,128)S(1)}, u32[]{:S(2)}, u32[]{:S(2)}) collective-permute-start(f32[1,8,16,256]{3,2,1,0:T(8,128)S(1)} %bitcast.378), channel_id=1, source_target_pairs={{8,0},{16,8},{24,16},{32,24},{40,32},{48,40},{56,48},{64,56},{72,6... | collective-permute-start | bytes 393224 | tf_op jit(solution)/shard_map/ppermute | solution.py:24
  119.9 5.9 %collective-permute-start.6 = (f32[1,8,16,256]{3,2,1,0:T(8,128)S(1)}, f32[1,8,16,256]{3,2,1,0:T(8,128)S(1)}, u32[]{:S(2)}, u32[]{:S(2)}) collective-permute-start(f32[1,8,16,256]{3,2,1,0:T(8,128)S(1)} %bitcast.381), channel_id=1, source_target_pairs={{8,0},{16,8},{24,16},{32,24},{40,32},{48,40},{56,48},{64,56},{72,6... | collective-permute-start | bytes 393224 | tf_op jit(solution)/shard_map/ppermute | solution.py:24
  130.8 5.9 %collective-permute-start.8 = (f32[1,8,16,256]{3,2,1,0:T(8,128)S(1)}, f32[1,8,16,256]{3,2,1,0:T(8,128)S(1)}, u32[]{:S(2)}, u32[]{:S(2)}) collective-permute-start(f32[1,8,16,256]{3,2,1,0:T(8,128)S(1)} %bitcast.389), channel_id=1, source_target_pairs={{8,0},{16,8},{24,16},{32,24},{40,32},{48,40},{56,48},{64,56},{72,6... | collective-permute-start | bytes 393224 | tf_op jit(solution)/shard_map/ppermute | solution.py:24
  143.8 20.2 %all_to_all.55 = f32[8,256,128]{2,1,0:T(8,128)} all-to-all(f32[8,256,128]{2,1,0:T(8,128)S(1)} %reshape.205), channel_id=1, replica_groups=mesh['gx_0'=8,'gx_1'=4,'gx_2'=2,'vert'=8] {'gx_1','gx_2'}, dimensions={0} | all-to-all | bytes 2097152 | tf_op jit(solution)/shard_map/all_to_all | solution.py:131
  165.3 14.4 %all_to_all.56 = f32[8,32,128]{2,1,0:T(8,128)S(1)} all-to-all(f32[8,32,128]{2,1,0:T(8,128)S(1)} %bitcast.391), channel_id=1, replica_groups=mesh['gx_0'=8,'gx_1'=4,'gx_2'=2,'vert'=8] {'gx_0'}, dimensions={0} | all-to-all | bytes 262144 | tf_op jit(solution)/shard_map/all_to_all | solution.py:131
  179.8 11.5 %all_to_all.57 = f32[8,32,128]{2,1,0:T(8,128)S(1)} all-to-all(f32[8,32,128]{2,1,0:T(8,128)S(1)} %broadcast_in_dim.24), channel_id=1, replica_groups=mesh['gx_0'=8,'gx_1'=4,'gx_2'=2,'vert'=8] {'gx_0'}, dimensions={0} | all-to-all | bytes 262144 | tf_op jit(solution)/shard_map/all_to_all | solution.py:134
  191.3 18.4 %all_to_all.58 = f32[8,256,128]{2,1,0:T(8,128)S(1)} all-to-all(f32[8,256,128]{2,1,0:T(8,128)S(1)} %broadcast_in_dim.26), channel_id=1, replica_groups=mesh['gx_0'=8,'gx_1'=4,'gx_2'=2,'vert'=8] {'gx_1','gx_2'}, dimensions={0} | all-to-all | bytes 2097152 | tf_op jit(solution)/shard_map/all_to_all | solution.py:134
  235.1 5.8 %collective-permute-start.12 = (f32[1,1,128,256]{3,2,1,0:T(8,128)S(1)}, f32[1,1,128,256]{3,2,1,0:T(8,128)S(1)}, u32[]{:S(2)}, u32[]{:S(2)}) collective-permute-start(f32[1,1,128,256]{3,2,1,0:T(8,128)S(1)} %bitcast.372), channel_id=1, source_target_pairs={{8,0},{16,8},{24,16},{32,24},{40,32},{48,40},{56,48},{64,56},{72,6... | collective-permute-start | bytes 393224 | tf_op jit(solution)/shard_map/ppermute | solution.py:38
  240.8 2.5 collective-permute-start.11
  245.8 4.4 %collective-permute-done.10 = f32[1,1,128,256]{3,2,1,0:T(8,128)S(1)} collective-permute-done((f32[1,1,128,256]{3,2,1,0:T(8,128)S(1)}, f32[1,1,128,256]{3,2,1,0:T(8,128)S(1)}, u32[]{:S(2)}, u32[]{:S(2)}) %collective-permute-start.10) | collective-permute-done | bytes 131104 | tf_op jit(solution)/shard_map/ppermute | solution.py:38
  254.0 5.8 %collective-permute-start.16 = (f32[1,1,128,256]{3,2,1,0:T(8,128)S(1)}, f32[1,1,128,256]{3,2,1,0:T(8,128)S(1)}, u32[]{:S(2)}, u32[]{:S(2)}) collective-permute-start(f32[1,1,128,256]{3,2,1,0:T(8,128)S(1)} %bitcast.384), channel_id=1, source_target_pairs={{8,0},{16,8},{24,16},{32,24},{40,32},{48,40},{56,48},{64,56},{72,6... | collective-permute-start | bytes 393224 | tf_op jit(solution)/shard_map/ppermute | solution.py:38
  260.7 2.3 collective-permute-start.15
  265.5 4.4 %collective-permute-done.14 = f32[1,1,128,256]{3,2,1,0:T(8,128)S(1)} collective-permute-done((f32[1,1,128,256]{3,2,1,0:T(8,128)S(1)}, f32[1,1,128,256]{3,2,1,0:T(8,128)S(1)}, u32[]{:S(2)}, u32[]{:S(2)}) %collective-permute-start.14) | collective-permute-done | bytes 131104 | tf_op jit(solution)/shard_map/ppermute | solution.py:38
  (133 shorter events, 72.4 us)
Async XLA Ops:
  0.6 88.6 %copy-start = (f32[256,256]{1,0:T(8,128)S(1)}, f32[256,256]{1,0:T(8,128)}, u32[]{:S(2)}) copy-start(f32[256,256]{1,0:T(8,128)} %param.5) | copy-start | bytes 786436
  0.6 6.2 %collective-permute-start.3 = (f32[1,1,128,256]{3,2,1,0:T(8,128)}, f32[1,1,128,256]{3,2,1,0:T(8,128)S(1)}, u32[]{:S(2)}, u32[]{:S(2)}) collective-permute-start(f32[1,1,128,256]{3,2,1,0:T(8,128)} %param.6), channel_id=1, source_target_pairs={{8,0},{16,8},{24,16},{32,24},{40,32},{48,40},{56,48},{64,56},{72,6... | collective-permute-start | bytes 393224 | tf_op jit(solution)/shard_map/ppermute | solution.py:52
  4.0 7.1 %collective-permute-start.2 = (f32[1,1,128,256]{3,2,1,0:T(8,128)}, f32[1,1,128,256]{3,2,1,0:T(8,128)S(1)}, u32[]{:S(2)}, u32[]{:S(2)}) collective-permute-start(f32[1,1,128,256]{3,2,1,0:T(8,128)} %param.6), channel_id=1, source_target_pairs={{1,0},{2,1},{3,2},{4,3},{5,4},{6,5},{7,6},{9,8},{10,9},{11,10},{12... | collective-permute-start | bytes 393224 | tf_op jit(solution)/shard_map/ppermute | solution.py:52
  31.5 57.8 %copy-start.4 = (f32[1,8,16,256]{3,2,1,0:T(8,128)S(1)}, f32[1,8,16,256]{3,2,1,0:T(8,128)}, u32[]{:S(2)}) copy-start(f32[1,8,16,256]{3,2,1,0:T(8,128)} %param.4) | copy-start | bytes 393220
  85.7 17.7 %all-to-all-start.5 = ((f32[8,192,128]{2,1,0:T(8,128)}), f32[8,192,128]{2,1,0:T(8,128)S(1)}, u32[]{:S(2)}, u32[]{:S(2)}) async-start(f32[8,192,128]{2,1,0:T(8,128)} %broadcast_in_dim.22), calls=%async_computation.5 | async-start | bytes 1572864 | tf_op jit(solution)/shard_map/all_to_all | solution.py:134
  89.5 8.5 %collective-permute-start.1 = (f32[1,8,16,256]{3,2,1,0:T(8,128)S(1)}, f32[1,8,16,256]{3,2,1,0:T(8,128)S(1)}, u32[]{:S(2)}, u32[]{:S(2)}) collective-permute-start(f32[1,8,16,256]{3,2,1,0:T(8,128)S(1)} %bitcast.368), channel_id=1, source_target_pairs={{0,8},{8,16},{16,24},{24,32},{32,40},{40,48},{48,56},{56,64},{64,7... | collective-permute-start | bytes 393224 | tf_op jit(solution)/shard_map/ppermute | solution.py:21
  91.8 8.2 %collective-permute-start = (f32[1,8,16,256]{3,2,1,0:T(8,128)S(1)}, f32[1,8,16,256]{3,2,1,0:T(8,128)S(1)}, u32[]{:S(2)}, u32[]{:S(2)}) collective-permute-start(f32[1,8,16,256]{3,2,1,0:T(8,128)S(1)} %bitcast.369), channel_id=1, source_target_pairs={{8,0},{16,8},{24,16},{32,24},{40,32},{48,40},{56,48},{64,56},{72,6... | collective-permute-start | bytes 393224 | tf_op jit(solution)/shard_map/ppermute | solution.py:24
  104.8 1.3 copy-start.5
  107.2 8.4 %collective-permute-start.5 = (f32[1,8,16,256]{3,2,1,0:T(8,128)S(1)}, f32[1,8,16,256]{3,2,1,0:T(8,128)S(1)}, u32[]{:S(2)}, u32[]{:S(2)}) collective-permute-start(f32[1,8,16,256]{3,2,1,0:T(8,128)S(1)} %bitcast.377), channel_id=1, source_target_pairs={{0,8},{8,16},{16,24},{24,32},{32,40},{40,48},{48,56},{56,64},{64,7... | collective-permute-start | bytes 393224 | tf_op jit(solution)/shard_map/ppermute | solution.py:21
  109.1 8.3 %collective-permute-start.4 = (f32[1,8,16,256]{3,2,1,0:T(8,128)S(1)}, f32[1,8,16,256]{3,2,1,0:T(8,128)S(1)}, u32[]{:S(2)}, u32[]{:S(2)}) collective-permute-start(f32[1,8,16,256]{3,2,1,0:T(8,128)S(1)} %bitcast.378), channel_id=1, source_target_pairs={{8,0},{16,8},{24,16},{32,24},{40,32},{48,40},{56,48},{64,56},{72,6... | collective-permute-start | bytes 393224 | tf_op jit(solution)/shard_map/ppermute | solution.py:24
  117.9 8.5 %collective-permute-start.7 = (f32[1,8,16,256]{3,2,1,0:T(8,128)S(1)}, f32[1,8,16,256]{3,2,1,0:T(8,128)S(1)}, u32[]{:S(2)}, u32[]{:S(2)}) collective-permute-start(f32[1,8,16,256]{3,2,1,0:T(8,128)S(1)} %bitcast.380), channel_id=1, source_target_pairs={{0,8},{8,16},{16,24},{24,32},{32,40},{40,48},{48,56},{56,64},{64,7... | collective-permute-start | bytes 393224 | tf_op jit(solution)/shard_map/ppermute | solution.py:21
  119.9 8.4 %collective-permute-start.6 = (f32[1,8,16,256]{3,2,1,0:T(8,128)S(1)}, f32[1,8,16,256]{3,2,1,0:T(8,128)S(1)}, u32[]{:S(2)}, u32[]{:S(2)}) collective-permute-start(f32[1,8,16,256]{3,2,1,0:T(8,128)S(1)} %bitcast.381), channel_id=1, source_target_pairs={{8,0},{16,8},{24,16},{32,24},{40,32},{48,40},{56,48},{64,56},{72,6... | collective-permute-start | bytes 393224 | tf_op jit(solution)/shard_map/ppermute | solution.py:24
  128.8 10.2 %collective-permute-start.9 = (f32[1,8,16,256]{3,2,1,0:T(8,128)S(1)}, f32[1,8,16,256]{3,2,1,0:T(8,128)S(1)}, u32[]{:S(2)}, u32[]{:S(2)}) collective-permute-start(f32[1,8,16,256]{3,2,1,0:T(8,128)S(1)} %bitcast.388), channel_id=1, source_target_pairs={{0,8},{8,16},{16,24},{24,32},{32,40},{40,48},{48,56},{56,64},{64,7... | collective-permute-start | bytes 393224 | tf_op jit(solution)/shard_map/ppermute | solution.py:21
  130.8 8.4 %collective-permute-start.8 = (f32[1,8,16,256]{3,2,1,0:T(8,128)S(1)}, f32[1,8,16,256]{3,2,1,0:T(8,128)S(1)}, u32[]{:S(2)}, u32[]{:S(2)}) collective-permute-start(f32[1,8,16,256]{3,2,1,0:T(8,128)S(1)} %bitcast.389), channel_id=1, source_target_pairs={{8,0},{16,8},{24,16},{32,24},{40,32},{48,40},{56,48},{64,56},{72,6... | collective-permute-start | bytes 393224 | tf_op jit(solution)/shard_map/ppermute | solution.py:24
  209.7 1.0 copy-start.2
  219.9 1.6 copy-start.3
  233.2 11.5 %collective-permute-start.13 = (f32[1,1,128,256]{3,2,1,0:T(8,128)S(1)}, f32[1,1,128,256]{3,2,1,0:T(8,128)S(1)}, u32[]{:S(2)}, u32[]{:S(2)}) collective-permute-start(f32[1,1,128,256]{3,2,1,0:T(8,128)S(1)} %bitcast.371), channel_id=1, source_target_pairs={{0,8},{8,16},{16,24},{24,32},{32,40},{40,48},{48,56},{56,64},{64,7... | collective-permute-start | bytes 393224 | tf_op jit(solution)/shard_map/ppermute | solution.py:37
  235.1 9.6 %collective-permute-start.12 = (f32[1,1,128,256]{3,2,1,0:T(8,128)S(1)}, f32[1,1,128,256]{3,2,1,0:T(8,128)S(1)}, u32[]{:S(2)}, u32[]{:S(2)}) collective-permute-start(f32[1,1,128,256]{3,2,1,0:T(8,128)S(1)} %bitcast.372), channel_id=1, source_target_pairs={{8,0},{16,8},{24,16},{32,24},{40,32},{48,40},{56,48},{64,56},{72,6... | collective-permute-start | bytes 393224 | tf_op jit(solution)/shard_map/ppermute | solution.py:38
  240.8 5.0 %collective-permute-start.11 = (f32[1,1,128,256]{3,2,1,0:T(8,128)S(1)}, f32[1,1,128,256]{3,2,1,0:T(8,128)S(1)}, u32[]{:S(2)}, u32[]{:S(2)}) collective-permute-start(f32[1,1,128,256]{3,2,1,0:T(8,128)S(1)} %bitcast.373), channel_id=1, source_target_pairs={{0,1},{1,2},{2,3},{3,4},{4,5},{5,6},{6,7},{8,9},{9,10},{10,11},{11... | collective-permute-start | bytes 393224 | tf_op jit(solution)/shard_map/ppermute | solution.py:37
  243.3 6.9 %collective-permute-start.10 = (f32[1,1,128,256]{3,2,1,0:T(8,128)S(1)}, f32[1,1,128,256]{3,2,1,0:T(8,128)S(1)}, u32[]{:S(2)}, u32[]{:S(2)}) collective-permute-start(f32[1,1,128,256]{3,2,1,0:T(8,128)S(1)} %bitcast.374), channel_id=1, source_target_pairs={{1,0},{2,1},{3,2},{4,3},{5,4},{6,5},{7,6},{9,8},{10,9},{11,10},{12... | collective-permute-start | bytes 393224 | tf_op jit(solution)/shard_map/ppermute | solution.py:38
  252.1 12.3 %collective-permute-start.17 = (f32[1,1,128,256]{3,2,1,0:T(8,128)S(1)}, f32[1,1,128,256]{3,2,1,0:T(8,128)S(1)}, u32[]{:S(2)}, u32[]{:S(2)}) collective-permute-start(f32[1,1,128,256]{3,2,1,0:T(8,128)S(1)} %bitcast.383), channel_id=1, source_target_pairs={{0,8},{8,16},{16,24},{24,32},{32,40},{40,48},{48,56},{56,64},{64,7... | collective-permute-start | bytes 393224 | tf_op jit(solution)/shard_map/ppermute | solution.py:37
  254.0 10.4 %collective-permute-start.16 = (f32[1,1,128,256]{3,2,1,0:T(8,128)S(1)}, f32[1,1,128,256]{3,2,1,0:T(8,128)S(1)}, u32[]{:S(2)}, u32[]{:S(2)}) collective-permute-start(f32[1,1,128,256]{3,2,1,0:T(8,128)S(1)} %bitcast.384), channel_id=1, source_target_pairs={{8,0},{16,8},{24,16},{32,24},{40,32},{48,40},{56,48},{64,56},{72,6... | collective-permute-start | bytes 393224 | tf_op jit(solution)/shard_map/ppermute | solution.py:38
  260.7 4.8 %collective-permute-start.15 = (f32[1,1,128,256]{3,2,1,0:T(8,128)S(1)}, f32[1,1,128,256]{3,2,1,0:T(8,128)S(1)}, u32[]{:S(2)}, u32[]{:S(2)}) collective-permute-start(f32[1,1,128,256]{3,2,1,0:T(8,128)S(1)} %bitcast.385), channel_id=1, source_target_pairs={{0,1},{1,2},{2,3},{3,4},{4,5},{5,6},{6,7},{8,9},{9,10},{10,11},{11... | collective-permute-start | bytes 393224 | tf_op jit(solution)/shard_map/ppermute | solution.py:37
  263.0 6.9 %collective-permute-start.14 = (f32[1,1,128,256]{3,2,1,0:T(8,128)S(1)}, f32[1,1,128,256]{3,2,1,0:T(8,128)S(1)}, u32[]{:S(2)}, u32[]{:S(2)}) collective-permute-start(f32[1,1,128,256]{3,2,1,0:T(8,128)S(1)} %bitcast.386), channel_id=1, source_target_pairs={{1,0},{2,1},{3,2},{4,3},{5,4},{6,5},{7,6},{9,8},{10,9},{11,10},{12... | collective-permute-start | bytes 393224 | tf_op jit(solution)/shard_map/ppermute | solution.py:38
  (1 other events, 0.9 us)

commit v2 on v1

--- a/solution.py
+++ b/solution.py
@@ -118,18 +118,31 @@
     return tuple(done)
 
 
+def doubled_total(part, axis, n):
+    if n & (n - 1):
+        return lax.psum(part, axis)
+    step = 1
+    while step < n:
+        pairs = [(i, i ^ step) for i in range(n)]
+        part = part + lax.ppermute(part, axis, pairs)
+        step *= 2
+    return part
+
+
 def staged_total(flat, axes):
     sizes = [lax.axis_size(a) for a in axes]
     devices = 1
     for n in sizes:
         devices *= n
     length = flat.shape[0]
-    piece = -(-length // (devices * 128)) * 128
+    piece = -(-length // (devices // sizes[-1] * 128)) * 128
+    devices = devices // sizes[-1]
     part = jnp.pad(flat, (0, piece * devices - length))
-    for axis, n in zip(axes, sizes):
+    for axis, n in zip(axes[:-1], sizes[:-1]):
         rows = part.reshape(n, -1, 128)
         part = jnp.sum(lax.all_to_all(rows, axis, 0, 0, tiled=True), axis=0).reshape(-1)
-    for axis, n in zip(axes[::-1], sizes[::-1]):
+    part = doubled_total(part, axes[-1], sizes[-1])
+    for axis, n in zip(axes[-2::-1], sizes[-2::-1]):
         rows = jnp.broadcast_to(part.reshape(1, -1, 128), (n, part.shape[0] // 128, 128))
         part = lax.all_to_all(rows, axis, 0, 0, tiled=True).reshape(-1)
     return part[:length]

time: 274 us -> 279 us (1.018)
  blocking collectives: 135 us -> 83.5 us
  starting transfers between devices: 61.9 us -> 93 us
  waiting for transfers between devices: 23.8 us -> 48.9 us
    ppermute x0 -> x6, starting transfers between devices: none -> 31.2 us  [doubled_total(): part = part + lax.ppermute(part, axis, pairs)]
    all_to_all x5 -> x3, blocking collectives: 83.4 us -> 54 us  [staged_total(): lax.all_to_all(rows, axis, 0, 0, tiled=True)]
    ppermute x0 -> x6, waiting for transfers between devices: none -> 25.1 us  [doubled_total(): part = part + lax.ppermute(part, axis, pairs)]
    all_to_all x4 -> x2, blocking collectives: 51.1 us -> 29.5 us  [staged_total(): part = lax.all_to_all(rows, axis, 0, 0, tiled=True).reshape(-1)]
  transfers between devices with their start and end apart: 19 -> 25, of which waited for: 13 -> 19; matrix products, arithmetic and copies ran while one was open for 3% -> 3% of each run, Pallas kernels for 0% -> 0%
where the time goes in v2:
time: 279 us; the launch traced here: 278 us
  starting transfers between devices  93 us (33%)
  blocking collectives  83.5 us (30%)
  waiting for transfers between devices  48.9 us (18%)
  matrix products  33.7 us (12%)
  local copies, waits for them, and re-layouts  12 us (4%)
  other arithmetic  4.02 us (1%)
    all_to_all x3, blocking collectives, staged_total(): lax.all_to_all(rows, axis, 0, 0, tiled=True)  54 us
    ppermute x6, starting transfers between devices, doubled_total(): part = part + lax.ppermute(part, axis, pairs)  31.2 us
    all_to_all x2, blocking collectives, staged_total(): part = lax.all_to_all(rows, axis, 0, 0, tiled=True).reshape(-1)  29.5 us
    ppermute x6, waiting for transfers between devices, doubled_total(): part = part + lax.ppermute(part, axis, pairs)  25.1 us
    ppermute x4, starting transfers between devices, padded_2(): lax.ppermute(lax.slice_in_dim(block, 0, width, axis=dim), axis, backward)  22.9 us
    ppermute x4, starting transfers between devices, extended(): lax.ppermute(first, axis, [(b, a) for a, b in up])  14.1 us
    ppermute x4, waiting for transfers between devices, extended(): lax.ppermute(first, axis, [(b, a) for a, b in up])  8.73 us
    ppermute x4, starting transfers between devices, extended(): lax.ppermute(last, axis, up)  8.65 us
  transfers between devices with their start and end apart: 25, of which 19 were waited for; matrix products, arithmetic and copies ran while one was open for 3% of the time, Pallas kernels for 0%

profile of v2, /device:TPU:64, one launch (start us, length us, event | category | flops | bytes accessed | tf_op | source)
XLA Modules:
  0.0 277.5 jit_solution(132056015095267857)
XLA Ops:
  0.6 3.3 %collective-permute-start.3 = (f32[1,1,128,256]{3,2,1,0:T(8,128)}, f32[1,1,128,256]{3,2,1,0:T(8,128)S(1)}, u32[]{:S(2)}, u32[]{:S(2)}) collective-permute-start(f32[1,1,128,256]{3,2,1,0:T(8,128)} %param.6), channel_id=1, source_target_pairs={{8,0},{16,8},{24,16},{32,24},{40,32},{48,40},{56,48},{64,56},{72,6... | collective-permute-start | bytes 393224 | tf_op jit(solution)/shard_map/ppermute | solution.py:52
  8.2 2.9 %collective-permute-done.2 = f32[1,1,128,256]{3,2,1,0:T(8,128)S(1)} collective-permute-done((f32[1,1,128,256]{3,2,1,0:T(8,128)}, f32[1,1,128,256]{3,2,1,0:T(8,128)S(1)}, u32[]{:S(2)}, u32[]{:S(2)}) %collective-permute-start.2) | collective-permute-done | bytes 131104 | tf_op jit(solution)/shard_map/ppermute | solution.py:52
  14.5 16.9 %all_to_all.30 = f32[8,192,128]{2,1,0:T(8,128)S(1)} all-to-all(f32[8,192,128]{2,1,0:T(8,128)S(1)} %reshape.207), channel_id=1, replica_groups=mesh['gx_0'=8,'gx_1'=4,'gx_2'=2,'vert'=8] {'gx_1','gx_2'}, dimensions={0} | all-to-all | bytes 1572864 | tf_op jit(solution)/shard_map/all_to_all | solution.py:143
  31.5 15.8 %all_to_all.31 = f32[8,24,128]{2,1,0:T(8,128)S(1)} all-to-all(f32[8,24,128]{2,1,0:T(8,128)S(1)} %bitcast.398), channel_id=1, replica_groups=mesh['gx_0'=8,'gx_1'=4,'gx_2'=2,'vert'=8] {'vert'}, dimensions={0} | all-to-all | bytes 196608 | tf_op jit(solution)/shard_map/all_to_all | solution.py:143
  49.2 3.7 %collective-permute-done.4 = f32[3072]{0:T(1024)S(1)} collective-permute-done((f32[3072]{0:T(1024)S(1)}, f32[3072]{0:T(1024)S(1)}, u32[]{:S(2)}, u32[]{:S(2)}) %collective-permute-start.4) | collective-permute-done | bytes 12320 | tf_op jit(solution)/shard_map/ppermute | solution.py:127
  52.9 6.5 %collective-permute-start.5 = (f32[3072]{0:T(1024)S(1)}, f32[3072]{0:T(1024)S(1)}, u32[]{:S(2)}, u32[]{:S(2)}) collective-permute-start(f32[3072]{0:T(1024)S(1)} %bitcast_add_fusion.4), channel_id=1, source_target_pairs={{0,128},{64,192},{128,0},{192,64},{256,384},{320,448},{384,256},{4... | collective-permute-start | bytes 36872 | tf_op jit(solution)/shard_map/ppermute | solution.py:127
  61.0 8.3 %collective-permute-start.6 = (f32[3072]{0:T(1024)S(1)}, f32[3072]{0:T(1024)S(1)}, u32[]{:S(2)}, u32[]{:S(2)}) collective-permute-start(f32[3072]{0:T(1024)S(1)} %add.164), channel_id=1, source_target_pairs={{0,256},{64,320},{128,384},{192,448},{256,0},{320,64},{384,128},{4... | collective-permute-start | bytes 36872 | tf_op jit(solution)/shard_map/ppermute | solution.py:127
  71.0 11.1 %all_to_all.32 = f32[8,24,128]{2,1,0:T(8,128)S(1)} all-to-all(f32[8,24,128]{2,1,0:T(8,128)S(1)} %broadcast_in_dim.15), channel_id=1, replica_groups=mesh['gx_0'=8,'gx_1'=4,'gx_2'=2,'vert'=8] {'vert'}, dimensions={0} | all-to-all | bytes 196608 | tf_op jit(solution)/shard_map/all_to_all | solution.py:147
  83.1 3.5 %all-to-all-start.3 = ((f32[8,192,128]{2,1,0:T(8,128)}), f32[8,192,128]{2,1,0:T(8,128)S(1)}, u32[]{:S(2)}, u32[]{:S(2)}) async-start(f32[8,192,128]{2,1,0:T(8,128)} %broadcast_in_dim.17), calls=%async_computation.3 | async-start | bytes 1572864 | tf_op jit(solution)/shard_map/all_to_all | solution.py:147
  89.2 5.4 %collective-permute-start = (f32[1,8,16,256]{3,2,1,0:T(8,128)S(1)}, f32[1,8,16,256]{3,2,1,0:T(8,128)S(1)}, u32[]{:S(2)}, u32[]{:S(2)}) collective-permute-start(f32[1,8,16,256]{3,2,1,0:T(8,128)S(1)} %bitcast.375), channel_id=1, source_target_pairs={{8,0},{16,8},{24,16},{32,24},{40,32},{48,40},{56,48},{64,56},{72,6... | collective-permute-start | bytes 393224 | tf_op jit(solution)/shard_map/ppermute | solution.py:24
  97.5 3.3 %all-to-all-done.3 = f32[8,192,128]{2,1,0:T(8,128)S(1)} async-done(((f32[8,192,128]{2,1,0:T(8,128)}), f32[8,192,128]{2,1,0:T(8,128)S(1)}, u32[]{:S(2)}, u32[]{:S(2)}) %all-to-all-start.3) | async-done | bytes 786464 | tf_op jit(solution)/shard_map/all_to_all | solution.py:147
  106.5 5.8 %collective-permute-start.7 = (f32[1,8,16,256]{3,2,1,0:T(8,128)S(1)}, f32[1,8,16,256]{3,2,1,0:T(8,128)S(1)}, u32[]{:S(2)}, u32[]{:S(2)}) collective-permute-start(f32[1,8,16,256]{3,2,1,0:T(8,128)S(1)} %bitcast.384), channel_id=1, source_target_pairs={{8,0},{16,8},{24,16},{32,24},{40,32},{48,40},{56,48},{64,56},{72,6... | collective-permute-start | bytes 393224 | tf_op jit(solution)/shard_map/ppermute | solution.py:24
  117.2 5.9 %collective-permute-start.9 = (f32[1,8,16,256]{3,2,1,0:T(8,128)S(1)}, f32[1,8,16,256]{3,2,1,0:T(8,128)S(1)}, u32[]{:S(2)}, u32[]{:S(2)}) collective-permute-start(f32[1,8,16,256]{3,2,1,0:T(8,128)S(1)} %bitcast.387), channel_id=1, source_target_pairs={{8,0},{16,8},{24,16},{32,24},{40,32},{48,40},{56,48},{64,56},{72,6... | collective-permute-start | bytes 393224 | tf_op jit(solution)/shard_map/ppermute | solution.py:24
  128.1 5.9 %collective-permute-start.11 = (f32[1,8,16,256]{3,2,1,0:T(8,128)S(1)}, f32[1,8,16,256]{3,2,1,0:T(8,128)S(1)}, u32[]{:S(2)}, u32[]{:S(2)}) collective-permute-start(f32[1,8,16,256]{3,2,1,0:T(8,128)S(1)} %bitcast.395), channel_id=1, source_target_pairs={{8,0},{16,8},{24,16},{32,24},{40,32},{48,40},{56,48},{64,56},{72,6... | collective-permute-start | bytes 393224 | tf_op jit(solution)/shard_map/ppermute | solution.py:24
  142.2 21.4 %all_to_all.33 = f32[8,256,128]{2,1,0:T(8,128)S(1)} all-to-all(f32[8,256,128]{2,1,0:T(8,128)} %reshape.212), channel_id=1, replica_groups=mesh['gx_0'=8,'gx_1'=4,'gx_2'=2,'vert'=8] {'gx_1','gx_2'}, dimensions={0} | all-to-all | bytes 2097152 | tf_op jit(solution)/shard_map/all_to_all | solution.py:143
  166.0 4.5 %collective-permute-done.13 = f32[32768]{0:T(1024)S(1)} collective-permute-done((f32[32768]{0:T(1024)S(1)}, f32[32768]{0:T(1024)S(1)}, u32[]{:S(2)}, u32[]{:S(2)}) %collective-permute-start.13) | collective-permute-done | bytes 131104 | tf_op jit(solution)/shard_map/ppermute | solution.py:127
  170.5 9.5 %collective-permute-start.14 = (f32[32768]{0:T(1024)S(1)}, f32[32768]{0:T(1024)S(1)}, u32[]{:S(2)}, u32[]{:S(2)}) collective-permute-start(f32[32768]{0:T(1024)S(1)} %bitcast_add_fusion.3), channel_id=1, source_target_pairs={{0,128},{64,192},{128,0},{192,64},{256,384},{320,448},{384,256},{4... | collective-permute-start | bytes 393224 | tf_op jit(solution)/shard_map/ppermute | solution.py:127
  180.1 4.0 %collective-permute-done.14 = f32[32768]{0:T(1024)S(1)} collective-permute-done((f32[32768]{0:T(1024)S(1)}, f32[32768]{0:T(1024)S(1)}, u32[]{:S(2)}, u32[]{:S(2)}) %collective-permute-start.14) | collective-permute-done | bytes 131104 | tf_op jit(solution)/shard_map/ppermute | solution.py:127
  186.7 9.6 %collective-permute-done.15 = f32[32768]{0:T(1024)S(1)} collective-permute-done((f32[32768]{0:T(1024)S(1)}, f32[32768]{0:T(1024)S(1)}, u32[]{:S(2)}, u32[]{:S(2)}) %collective-permute-start.15) | collective-permute-done | bytes 131104 | tf_op jit(solution)/shard_map/ppermute | solution.py:127
  196.4 18.4 %all_to_all.34 = f32[8,256,128]{2,1,0:T(8,128)S(1)} all-to-all(f32[8,256,128]{2,1,0:T(8,128)S(1)} %broadcast_in_dim.20), channel_id=1, replica_groups=mesh['gx_0'=8,'gx_1'=4,'gx_2'=2,'vert'=8] {'gx_1','gx_2'}, dimensions={0} | all-to-all | bytes 2097152 | tf_op jit(solution)/shard_map/all_to_all | solution.py:147
  240.2 5.8 %collective-permute-start.18 = (f32[1,1,128,256]{3,2,1,0:T(8,128)S(1)}, f32[1,1,128,256]{3,2,1,0:T(8,128)S(1)}, u32[]{:S(2)}, u32[]{:S(2)}) collective-permute-start(f32[1,1,128,256]{3,2,1,0:T(8,128)S(1)} %bitcast.378), channel_id=1, source_target_pairs={{8,0},{16,8},{24,16},{32,24},{40,32},{48,40},{56,48},{64,56},{72,6... | collective-permute-start | bytes 393224 | tf_op jit(solution)/shard_map/ppermute | solution.py:38
  250.9 4.4 %collective-permute-done.16 = f32[1,1,128,256]{3,2,1,0:T(8,128)S(1)} collective-permute-done((f32[1,1,128,256]{3,2,1,0:T(8,128)S(1)}, f32[1,1,128,256]{3,2,1,0:T(8,128)S(1)}, u32[]{:S(2)}, u32[]{:S(2)}) %collective-permute-start.16) | collective-permute-done | bytes 131104 | tf_op jit(solution)/shard_map/ppermute | solution.py:38
  259.1 5.8 %collective-permute-start.22 = (f32[1,1,128,256]{3,2,1,0:T(8,128)S(1)}, f32[1,1,128,256]{3,2,1,0:T(8,128)S(1)}, u32[]{:S(2)}, u32[]{:S(2)}) collective-permute-start(f32[1,1,128,256]{3,2,1,0:T(8,128)S(1)} %bitcast.390), channel_id=1, source_target_pairs={{8,0},{16,8},{24,16},{32,24},{40,32},{48,40},{56,48},{64,56},{72,6... | collective-permute-start | bytes 393224 | tf_op jit(solution)/shard_map/ppermute | solution.py:38
  270.6 4.4 %collective-permute-done.20 = f32[1,1,128,256]{3,2,1,0:T(8,128)S(1)} collective-permute-done((f32[1,1,128,256]{3,2,1,0:T(8,128)S(1)}, f32[1,1,128,256]{3,2,1,0:T(8,128)S(1)}, u32[]{:S(2)}, u32[]{:S(2)}) %collective-permute-start.20) | collective-permute-done | bytes 131104 | tf_op jit(solution)/shard_map/ppermute | solution.py:38
  (141 shorter events, 89.4 us)
Async XLA Ops:
  0.6 6.2 %collective-permute-start.3 = (f32[1,1,128,256]{3,2,1,0:T(8,128)}, f32[1,1,128,256]{3,2,1,0:T(8,128)S(1)}, u32[]{:S(2)}, u32[]{:S(2)}) collective-permute-start(f32[1,1,128,256]{3,2,1,0:T(8,128)} %param.6), channel_id=1, source_target_pairs={{8,0},{16,8},{24,16},{32,24},{40,32},{48,40},{56,48},{64,56},{72,6... | collective-permute-start | bytes 393224 | tf_op jit(solution)/shard_map/ppermute | solution.py:52
  4.0 7.1 %collective-permute-start.2 = (f32[1,1,128,256]{3,2,1,0:T(8,128)}, f32[1,1,128,256]{3,2,1,0:T(8,128)S(1)}, u32[]{:S(2)}, u32[]{:S(2)}) collective-permute-start(f32[1,1,128,256]{3,2,1,0:T(8,128)} %param.6), channel_id=1, source_target_pairs={{1,0},{2,1},{3,2},{4,3},{5,4},{6,5},{7,6},{9,8},{10,9},{11,10},{12... | collective-permute-start | bytes 393224 | tf_op jit(solution)/shard_map/ppermute | solution.py:52
  47.3 5.6 %collective-permute-start.4 = (f32[3072]{0:T(1024)S(1)}, f32[3072]{0:T(1024)S(1)}, u32[]{:S(2)}, u32[]{:S(2)}) collective-permute-start(f32[3072]{0:T(1024)S(1)} %bitcast.404), channel_id=1, source_target_pairs={{0,64},{64,0},{128,192},{192,128},{256,320},{320,256},{384,448},{4... | collective-permute-start | bytes 36872 | tf_op jit(solution)/shard_map/ppermute | solution.py:127
  52.9 8.1 %collective-permute-start.5 = (f32[3072]{0:T(1024)S(1)}, f32[3072]{0:T(1024)S(1)}, u32[]{:S(2)}, u32[]{:S(2)}) collective-permute-start(f32[3072]{0:T(1024)S(1)} %bitcast_add_fusion.4), channel_id=1, source_target_pairs={{0,128},{64,192},{128,0},{192,64},{256,384},{320,448},{384,256},{4... | collective-permute-start | bytes 36872 | tf_op jit(solution)/shard_map/ppermute | solution.py:127
  61.0 10.0 %collective-permute-start.6 = (f32[3072]{0:T(1024)S(1)}, f32[3072]{0:T(1024)S(1)}, u32[]{:S(2)}, u32[]{:S(2)}) collective-permute-start(f32[3072]{0:T(1024)S(1)} %add.164), channel_id=1, source_target_pairs={{0,256},{64,320},{128,384},{192,448},{256,0},{320,64},{384,128},{4... | collective-permute-start | bytes 36872 | tf_op jit(solution)/shard_map/ppermute | solution.py:127
  83.1 17.7 %all-to-all-start.3 = ((f32[8,192,128]{2,1,0:T(8,128)}), f32[8,192,128]{2,1,0:T(8,128)S(1)}, u32[]{:S(2)}, u32[]{:S(2)}) async-start(f32[8,192,128]{2,1,0:T(8,128)} %broadcast_in_dim.17), calls=%async_computation.3 | async-start | bytes 1572864 | tf_op jit(solution)/shard_map/all_to_all | solution.py:147
  86.9 8.5 %collective-permute-start.1 = (f32[1,8,16,256]{3,2,1,0:T(8,128)S(1)}, f32[1,8,16,256]{3,2,1,0:T(8,128)S(1)}, u32[]{:S(2)}, u32[]{:S(2)}) collective-permute-start(f32[1,8,16,256]{3,2,1,0:T(8,128)S(1)} %bitcast.374), channel_id=1, source_target_pairs={{0,8},{8,16},{16,24},{24,32},{32,40},{40,48},{48,56},{56,64},{64,7... | collective-permute-start | bytes 393224 | tf_op jit(solution)/shard_map/ppermute | solution.py:21
  89.2 8.2 %collective-permute-start = (f32[1,8,16,256]{3,2,1,0:T(8,128)S(1)}, f32[1,8,16,256]{3,2,1,0:T(8,128)S(1)}, u32[]{:S(2)}, u32[]{:S(2)}) collective-permute-start(f32[1,8,16,256]{3,2,1,0:T(8,128)S(1)} %bitcast.375), channel_id=1, source_target_pairs={{8,0},{16,8},{24,16},{32,24},{40,32},{48,40},{56,48},{64,56},{72,6... | collective-permute-start | bytes 393224 | tf_op jit(solution)/shard_map/ppermute | solution.py:24
  104.6 8.4 %collective-permute-start.8 = (f32[1,8,16,256]{3,2,1,0:T(8,128)S(1)}, f32[1,8,16,256]{3,2,1,0:T(8,128)S(1)}, u32[]{:S(2)}, u32[]{:S(2)}) collective-permute-start(f32[1,8,16,256]{3,2,1,0:T(8,128)S(1)} %bitcast.383), channel_id=1, source_target_pairs={{0,8},{8,16},{16,24},{24,32},{32,40},{40,48},{48,56},{56,64},{64,7... | collective-permute-start | bytes 393224 | tf_op jit(solution)/shard_map/ppermute | solution.py:21
  106.5 8.3 %collective-permute-start.7 = (f32[1,8,16,256]{3,2,1,0:T(8,128)S(1)}, f32[1,8,16,256]{3,2,1,0:T(8,128)S(1)}, u32[]{:S(2)}, u32[]{:S(2)}) collective-permute-start(f32[1,8,16,256]{3,2,1,0:T(8,128)S(1)} %bitcast.384), channel_id=1, source_target_pairs={{8,0},{16,8},{24,16},{32,24},{40,32},{48,40},{56,48},{64,56},{72,6... | collective-permute-start | bytes 393224 | tf_op jit(solution)/shard_map/ppermute | solution.py:24
  115.3 8.5 %collective-permute-start.10 = (f32[1,8,16,256]{3,2,1,0:T(8,128)S(1)}, f32[1,8,16,256]{3,2,1,0:T(8,128)S(1)}, u32[]{:S(2)}, u32[]{:S(2)}) collective-permute-start(f32[1,8,16,256]{3,2,1,0:T(8,128)S(1)} %bitcast.386), channel_id=1, source_target_pairs={{0,8},{8,16},{16,24},{24,32},{32,40},{40,48},{48,56},{56,64},{64,7... | collective-permute-start | bytes 393224 | tf_op jit(solution)/shard_map/ppermute | solution.py:21
  117.2 8.4 %collective-permute-start.9 = (f32[1,8,16,256]{3,2,1,0:T(8,128)S(1)}, f32[1,8,16,256]{3,2,1,0:T(8,128)S(1)}, u32[]{:S(2)}, u32[]{:S(2)}) collective-permute-start(f32[1,8,16,256]{3,2,1,0:T(8,128)S(1)} %bitcast.387), channel_id=1, source_target_pairs={{8,0},{16,8},{24,16},{32,24},{40,32},{48,40},{56,48},{64,56},{72,6... | collective-permute-start | bytes 393224 | tf_op jit(solution)/shard_map/ppermute | solution.py:24
  126.2 10.2 %collective-permute-start.12 = (f32[1,8,16,256]{3,2,1,0:T(8,128)S(1)}, f32[1,8,16,256]{3,2,1,0:T(8,128)S(1)}, u32[]{:S(2)}, u32[]{:S(2)}) collective-permute-start(f32[1,8,16,256]{3,2,1,0:T(8,128)S(1)} %bitcast.394), channel_id=1, source_target_pairs={{0,8},{8,16},{16,24},{24,32},{32,40},{40,48},{48,56},{56,64},{64,7... | collective-permute-start | bytes 393224 | tf_op jit(solution)/shard_map/ppermute | solution.py:21
  128.1 8.4 %collective-permute-start.11 = (f32[1,8,16,256]{3,2,1,0:T(8,128)S(1)}, f32[1,8,16,256]{3,2,1,0:T(8,128)S(1)}, u32[]{:S(2)}, u32[]{:S(2)}) collective-permute-start(f32[1,8,16,256]{3,2,1,0:T(8,128)S(1)} %bitcast.395), channel_id=1, source_target_pairs={{8,0},{16,8},{24,16},{32,24},{40,32},{48,40},{56,48},{64,56},{72,6... | collective-permute-start | bytes 393224 | tf_op jit(solution)/shard_map/ppermute | solution.py:24
  163.6 6.9 %collective-permute-start.13 = (f32[32768]{0:T(1024)S(1)}, f32[32768]{0:T(1024)S(1)}, u32[]{:S(2)}, u32[]{:S(2)}) collective-permute-start(f32[32768]{0:T(1024)S(1)} %bitcast.397), channel_id=1, source_target_pairs={{0,64},{64,0},{128,192},{192,128},{256,320},{320,256},{384,448},{4... | collective-permute-start | bytes 393224 | tf_op jit(solution)/shard_map/ppermute | solution.py:127
  170.5 13.6 %collective-permute-start.14 = (f32[32768]{0:T(1024)S(1)}, f32[32768]{0:T(1024)S(1)}, u32[]{:S(2)}, u32[]{:S(2)}) collective-permute-start(f32[32768]{0:T(1024)S(1)} %bitcast_add_fusion.3), channel_id=1, source_target_pairs={{0,128},{64,192},{128,0},{192,64},{256,384},{320,448},{384,256},{4... | collective-permute-start | bytes 393224 | tf_op jit(solution)/shard_map/ppermute | solution.py:127
  184.1 12.2 %collective-permute-start.15 = (f32[32768]{0:T(1024)S(1)}, f32[32768]{0:T(1024)S(1)}, u32[]{:S(2)}, u32[]{:S(2)}) collective-permute-start(f32[32768]{0:T(1024)S(1)} %add.181), channel_id=1, source_target_pairs={{0,256},{64,320},{128,384},{192,448},{256,0},{320,64},{384,128},{4... | collective-permute-start | bytes 393224 | tf_op jit(solution)/shard_map/ppermute | solution.py:127
  238.2 11.5 %collective-permute-start.19 = (f32[1,1,128,256]{3,2,1,0:T(8,128)S(1)}, f32[1,1,128,256]{3,2,1,0:T(8,128)S(1)}, u32[]{:S(2)}, u32[]{:S(2)}) collective-permute-start(f32[1,1,128,256]{3,2,1,0:T(8,128)S(1)} %bitcast.377), channel_id=1, source_target_pairs={{0,8},{8,16},{16,24},{24,32},{32,40},{40,48},{48,56},{56,64},{64,7... | collective-permute-start | bytes 393224 | tf_op jit(solution)/shard_map/ppermute | solution.py:37
  240.2 9.6 %collective-permute-start.18 = (f32[1,1,128,256]{3,2,1,0:T(8,128)S(1)}, f32[1,1,128,256]{3,2,1,0:T(8,128)S(1)}, u32[]{:S(2)}, u32[]{:S(2)}) collective-permute-start(f32[1,1,128,256]{3,2,1,0:T(8,128)S(1)} %bitcast.378), channel_id=1, source_target_pairs={{8,0},{16,8},{24,16},{32,24},{40,32},{48,40},{56,48},{64,56},{72,6... | collective-permute-start | bytes 393224 | tf_op jit(solution)/shard_map/ppermute | solution.py:38
  245.9 5.0 %collective-permute-start.17 = (f32[1,1,128,256]{3,2,1,0:T(8,128)S(1)}, f32[1,1,128,256]{3,2,1,0:T(8,128)S(1)}, u32[]{:S(2)}, u32[]{:S(2)}) collective-permute-start(f32[1,1,128,256]{3,2,1,0:T(8,128)S(1)} %bitcast.379), channel_id=1, source_target_pairs={{0,1},{1,2},{2,3},{3,4},{4,5},{5,6},{6,7},{8,9},{9,10},{10,11},{11... | collective-permute-start | bytes 393224 | tf_op jit(solution)/shard_map/ppermute | solution.py:37
  248.4 6.9 %collective-permute-start.16 = (f32[1,1,128,256]{3,2,1,0:T(8,128)S(1)}, f32[1,1,128,256]{3,2,1,0:T(8,128)S(1)}, u32[]{:S(2)}, u32[]{:S(2)}) collective-permute-start(f32[1,1,128,256]{3,2,1,0:T(8,128)S(1)} %bitcast.380), channel_id=1, source_target_pairs={{1,0},{2,1},{3,2},{4,3},{5,4},{6,5},{7,6},{9,8},{10,9},{11,10},{12... | collective-permute-start | bytes 393224 | tf_op jit(solution)/shard_map/ppermute | solution.py:38
  257.2 12.3 %collective-permute-start.23 = (f32[1,1,128,256]{3,2,1,0:T(8,128)S(1)}, f32[1,1,128,256]{3,2,1,0:T(8,128)S(1)}, u32[]{:S(2)}, u32[]{:S(2)}) collective-permute-start(f32[1,1,128,256]{3,2,1,0:T(8,128)S(1)} %bitcast.389), channel_id=1, source_target_pairs={{0,8},{8,16},{16,24},{24,32},{32,40},{40,48},{48,56},{56,64},{64,7... | collective-permute-start | bytes 393224 | tf_op jit(solution)/shard_map/ppermute | solution.py:37
  259.1 10.4 %collective-permute-start.22 = (f32[1,1,128,256]{3,2,1,0:T(8,128)S(1)}, f32[1,1,128,256]{3,2,1,0:T(8,128)S(1)}, u32[]{:S(2)}, u32[]{:S(2)}) collective-permute-start(f32[1,1,128,256]{3,2,1,0:T(8,128)S(1)} %bitcast.390), channel_id=1, source_target_pairs={{8,0},{16,8},{24,16},{32,24},{40,32},{48,40},{56,48},{64,56},{72,6... | collective-permute-start | bytes 393224 | tf_op jit(solution)/shard_map/ppermute | solution.py:38
  268.1 6.9 %collective-permute-start.20 = (f32[1,1,128,256]{3,2,1,0:T(8,128)S(1)}, f32[1,1,128,256]{3,2,1,0:T(8,128)S(1)}, u32[]{:S(2)}, u32[]{:S(2)}) collective-permute-start(f32[1,1,128,256]{3,2,1,0:T(8,128)S(1)} %bitcast.392), channel_id=1, source_target_pairs={{1,0},{2,1},{3,2},{4,3},{5,4},{6,5},{7,6},{9,8},{10,9},{11,10},{12... | collective-permute-start | bytes 393224 | tf_op jit(solution)/shard_map/ppermute | solution.py:38
  (7 other events, 150.8 us)

commit v3 on v1

--- a/solution.py
+++ b/solution.py
@@ -202,7 +202,9 @@
     identity = jnp.eye(gram_matrix.shape[0], dtype=jnp.float32)
     root_part = gram_matrix / frob_norm
     inv_root = identity
-    for sweep_index in range(NS_STEPS):
+
+    def sweep(_, carried):
+        root_part, inv_root = carried
         middle = 1.5 * identity - 0.5 * jnp.dot(
             inv_root, root_part, precision=HIGHEST, preferred_element_type=jnp.float32
         )
@@ -210,6 +212,9 @@
             root_part, middle, precision=HIGHEST, preferred_element_type=jnp.float32
         )
         inv_root = jnp.dot(middle, inv_root, precision=HIGHEST, preferred_element_type=jnp.float32)
+        return root_part, inv_root
+
+    root_part, inv_root = lax.fori_loop(0, NS_STEPS, sweep, (root_part, inv_root))
     scale_root = jnp.sqrt(frob_norm)
     return (inv_root / scale_root, root_part * scale_root)
 

time: 274 us -> 283 us (1.033)
  blocking collectives: 135 us -> 116 us
  waiting for transfers between devices: 23.8 us -> 39.4 us
  local copies, waits for them, and re-layouts: 11.1 us -> 15.1 us
  starting transfers between devices: 61.9 us -> 65.6 us
    all_to_all x4 -> x3, blocking collectives: 51.1 us -> 32.7 us  [staged_total(): part = lax.all_to_all(rows, axis, 0, 0, tiled=True).reshape(-1)]
    all_to_all x1 -> x2, waiting for transfers between devices: 3.3 us -> 19 us  [staged_total(): part = lax.all_to_all(rows, axis, 0, 0, tiled=True).reshape(-1)]
    all_to_all x1 -> x2, starting transfers between devices: 3.55 us -> 7.28 us  [staged_total(): part = lax.all_to_all(rows, axis, 0, 0, tiled=True).reshape(-1)]
  transfers between devices with their start and end apart: 19 -> 20, of which waited for: 13 -> 14; matrix products, arithmetic and copies ran while one was open for 3% -> 3% of each run, Pallas kernels for 0% -> 0%
where the time goes in v3:
time: 283 us; the launch traced here: 282 us
  blocking collectives  116 us (41%)
  starting transfers between devices  65.6 us (23%)
  waiting for transfers between devices  39.4 us (14%)
  matrix products  35.6 us (13%)
  local copies, waits for them, and re-layouts  15.1 us (5%)
  other arithmetic  7.25 us (3%)
    all_to_all x5, blocking collectives, staged_total(): lax.all_to_all(rows, axis, 0, 0, tiled=True)  83.4 us
    all_to_all x3, blocking collectives, staged_total(): part = lax.all_to_all(rows, axis, 0, 0, tiled=True).reshape(-1)  32.7 us
    ppermute x4, starting transfers between devices, padded_2(): lax.ppermute(lax.slice_in_dim(block, 0, width, axis=dim), axis, backward)  22.9 us
    all_to_all x2, waiting for transfers between devices, staged_total(): part = lax.all_to_all(rows, axis, 0, 0, tiled=True).reshape(-1)  19 us
    ppermute x4, starting transfers between devices, extended(): lax.ppermute(first, axis, [(b, a) for a, b in up])  14.1 us
    ppermute x4, waiting for transfers between devices, extended(): lax.ppermute(first, axis, [(b, a) for a, b in up])  8.73 us
    ppermute x4, starting transfers between devices, extended(): lax.ppermute(last, axis, up)  8.64 us
    ppermute x4, starting transfers between devices, padded_2(): lax.ppermute(lax.slice_in_dim(block, block.shape[dim] - width, None, axis...  8.06 us
  transfers between devices with their start and end apart: 20, of which 14 were waited for; matrix products, arithmetic and copies ran while one was open for 3% of the time, Pallas kernels for 0%

profile of v3, /device:TPU:64, one launch (start us, length us, event | category | flops | bytes accessed | tf_op | source)
XLA Modules:
  0.0 281.6 jit_solution(17832689356113352938)
XLA Ops:
  0.6 3.3 %collective-permute-start.3 = (f32[1,1,128,256]{3,2,1,0:T(8,128)}, f32[1,1,128,256]{3,2,1,0:T(8,128)S(1)}, u32[]{:S(2)}, u32[]{:S(2)}) collective-permute-start(f32[1,1,128,256]{3,2,1,0:T(8,128)} %param.8), channel_id=1, source_target_pairs={{8,0},{16,8},{24,16},{32,24},{40,32},{48,40},{56,48},{64,56},{72,6... | collective-permute-start | bytes 393224 | tf_op jit(solution)/shard_map/ppermute | solution.py:52
  8.2 2.9 %collective-permute-done.2 = f32[1,1,128,256]{3,2,1,0:T(8,128)S(1)} collective-permute-done((f32[1,1,128,256]{3,2,1,0:T(8,128)}, f32[1,1,128,256]{3,2,1,0:T(8,128)S(1)}, u32[]{:S(2)}, u32[]{:S(2)}) %collective-permute-start.2) | collective-permute-done | bytes 131104 | tf_op jit(solution)/shard_map/ppermute | solution.py:52
  14.5 16.9 %all_to_all.50 = f32[8,192,128]{2,1,0:T(8,128)S(1)} all-to-all(f32[8,192,128]{2,1,0:T(8,128)S(1)} %reshape.201), channel_id=1, replica_groups=mesh['gx_0'=8,'gx_1'=4,'gx_2'=2,'vert'=8] {'gx_1','gx_2'}, dimensions={0} | all-to-all | bytes 1572864 | tf_op jit(solution)/shard_map/all_to_all | solution.py:131
  31.5 15.8 %all_to_all.51 = f32[8,24,128]{2,1,0:T(8,128)S(1)} all-to-all(f32[8,24,128]{2,1,0:T(8,128)S(1)} %bitcast.367), channel_id=1, replica_groups=mesh['gx_0'=8,'gx_1'=4,'gx_2'=2,'vert'=8] {'vert'}, dimensions={0} | all-to-all | bytes 196608 | tf_op jit(solution)/shard_map/all_to_all | solution.py:131
  47.3 16.1 %all_to_all.52 = f32[8,3,128]{2,1,0:T(4,128)S(1)} all-to-all(f32[8,3,128]{2,1,0:T(4,128)S(1)} %reshape_reshape.9), channel_id=1, replica_groups=mesh['gx_0'=8,'gx_1'=4,'gx_2'=2,'vert'=8] {'gx_0'}, dimensions={0} | all-to-all | bytes 24576 | tf_op jit(solution)/shard_map/all_to_all | solution.py:131
  63.4 10.1 %all_to_all.53 = f32[8,3,128]{2,1,0:T(4,128)S(1)} all-to-all(f32[8,3,128]{2,1,0:T(4,128)S(1)} %broadcast_in_dim.18), channel_id=1, replica_groups=mesh['gx_0'=8,'gx_1'=4,'gx_2'=2,'vert'=8] {'gx_0'}, dimensions={0} | all-to-all | bytes 24576 | tf_op jit(solution)/shard_map/all_to_all | solution.py:134
  73.6 11.1 %all_to_all.54 = f32[8,24,128]{2,1,0:T(8,128)S(1)} all-to-all(f32[8,24,128]{2,1,0:T(8,128)S(1)} %broadcast_in_dim.20), channel_id=1, replica_groups=mesh['gx_0'=8,'gx_1'=4,'gx_2'=2,'vert'=8] {'vert'}, dimensions={0} | all-to-all | bytes 196608 | tf_op jit(solution)/shard_map/all_to_all | solution.py:134
  85.6 3.5 %all-to-all-start.5 = ((f32[8,192,128]{2,1,0:T(8,128)}), f32[8,192,128]{2,1,0:T(8,128)S(1)}, u32[]{:S(2)}, u32[]{:S(2)}) async-start(f32[8,192,128]{2,1,0:T(8,128)} %broadcast_in_dim.22), calls=%async_computation.5 | async-start | bytes 1572864 | tf_op jit(solution)/shard_map/all_to_all | solution.py:134
  91.8 5.4 %collective-permute-start = (f32[1,8,16,256]{3,2,1,0:T(8,128)S(1)}, f32[1,8,16,256]{3,2,1,0:T(8,128)S(1)}, u32[]{:S(2)}, u32[]{:S(2)}) collective-permute-start(f32[1,8,16,256]{3,2,1,0:T(8,128)S(1)} %bitcast.343), channel_id=1, source_target_pairs={{8,0},{16,8},{24,16},{32,24},{40,32},{48,40},{56,48},{64,56},{72,6... | collective-permute-start | bytes 393224 | tf_op jit(solution)/shard_map/ppermute | solution.py:24
  100.1 3.3 %all-to-all-done.5 = f32[8,192,128]{2,1,0:T(8,128)S(1)} async-done(((f32[8,192,128]{2,1,0:T(8,128)}), f32[8,192,128]{2,1,0:T(8,128)S(1)}, u32[]{:S(2)}, u32[]{:S(2)}) %all-to-all-start.5) | async-done | bytes 786464 | tf_op jit(solution)/shard_map/all_to_all | solution.py:134
  109.1 5.8 %collective-permute-start.4 = (f32[1,8,16,256]{3,2,1,0:T(8,128)S(1)}, f32[1,8,16,256]{3,2,1,0:T(8,128)S(1)}, u32[]{:S(2)}, u32[]{:S(2)}) collective-permute-start(f32[1,8,16,256]{3,2,1,0:T(8,128)S(1)} %bitcast.352), channel_id=1, source_target_pairs={{8,0},{16,8},{24,16},{32,24},{40,32},{48,40},{56,48},{64,56},{72,6... | collective-permute-start | bytes 393224 | tf_op jit(solution)/shard_map/ppermute | solution.py:24
  119.8 5.9 %collective-permute-start.6 = (f32[1,8,16,256]{3,2,1,0:T(8,128)S(1)}, f32[1,8,16,256]{3,2,1,0:T(8,128)S(1)}, u32[]{:S(2)}, u32[]{:S(2)}) collective-permute-start(f32[1,8,16,256]{3,2,1,0:T(8,128)S(1)} %bitcast.355), channel_id=1, source_target_pairs={{8,0},{16,8},{24,16},{32,24},{40,32},{48,40},{56,48},{64,56},{72,6... | collective-permute-start | bytes 393224 | tf_op jit(solution)/shard_map/ppermute | solution.py:24
  130.7 5.9 %collective-permute-start.8 = (f32[1,8,16,256]{3,2,1,0:T(8,128)S(1)}, f32[1,8,16,256]{3,2,1,0:T(8,128)S(1)}, u32[]{:S(2)}, u32[]{:S(2)}) collective-permute-start(f32[1,8,16,256]{3,2,1,0:T(8,128)S(1)} %bitcast.365), channel_id=1, source_target_pairs={{8,0},{16,8},{24,16},{32,24},{40,32},{48,40},{56,48},{64,56},{72,6... | collective-permute-start | bytes 393224 | tf_op jit(solution)/shard_map/ppermute | solution.py:24
  143.8 20.2 %all_to_all.55 = f32[8,256,128]{2,1,0:T(8,128)} all-to-all(f32[8,256,128]{2,1,0:T(8,128)S(1)} %reshape.205), channel_id=1, replica_groups=mesh['gx_0'=8,'gx_1'=4,'gx_2'=2,'vert'=8] {'gx_1','gx_2'}, dimensions={0} | all-to-all | bytes 2097152 | tf_op jit(solution)/shard_map/all_to_all | solution.py:131
  165.3 14.4 %all_to_all.56 = f32[8,32,128]{2,1,0:T(8,128)S(1)} all-to-all(f32[8,32,128]{2,1,0:T(8,128)S(1)} %bitcast.362), channel_id=1, replica_groups=mesh['gx_0'=8,'gx_1'=4,'gx_2'=2,'vert'=8] {'gx_0'}, dimensions={0} | all-to-all | bytes 262144 | tf_op jit(solution)/shard_map/all_to_all | solution.py:131
  179.7 11.5 %all_to_all.57 = f32[8,32,128]{2,1,0:T(8,128)S(1)} all-to-all(f32[8,32,128]{2,1,0:T(8,128)S(1)} %broadcast_in_dim.24), channel_id=1, replica_groups=mesh['gx_0'=8,'gx_1'=4,'gx_2'=2,'vert'=8] {'gx_0'}, dimensions={0} | all-to-all | bytes 262144 | tf_op jit(solution)/shard_map/all_to_all | solution.py:134
  192.3 3.7 %all-to-all-start.9 = ((f32[8,256,128]{2,1,0:T(8,128)}), f32[8,256,128]{2,1,0:T(8,128)S(1)}, u32[]{:S(2)}, u32[]{:S(2)}) async-start(f32[8,256,128]{2,1,0:T(8,128)} %broadcast_in_dim.26), calls=%async_computation.9 | async-start | bytes 2097152 | tf_op jit(solution)/shard_map/all_to_all | solution.py:134
  196.0 15.7 %all-to-all-done.9 = f32[8,256,128]{2,1,0:T(8,128)S(1)} async-done(((f32[8,256,128]{2,1,0:T(8,128)}), f32[8,256,128]{2,1,0:T(8,128)S(1)}, u32[]{:S(2)}, u32[]{:S(2)}) %all-to-all-start.9) | async-done | bytes 1048608 | tf_op jit(solution)/shard_map/all_to_all | solution.py:134
  221.2 11.8 %while.13 = (s32[]{:T(128)}, f32[256,256]{0,1:T(8,128)S(1)}, f32[256,256]{1,0:T(8,128)S(1)}, s32[]{:T(128)}) while((s32[]{:T(128)}, f32[256,256]{0,1:T(8,128)S(1)}, f32[256,256]{1,0:T(8,128)S(1)}, s32[]{:T(128)}) %tuple.31), condition=%wide.region_7.8_spmd.clone, body=%wide.region_6.7_spmd.clone.sunk | while | flops 604241920 | bytes 3407925 | solution.py:217
  244.2 5.8 %collective-permute-start.12 = (f32[1,1,128,256]{3,2,1,0:T(8,128)S(1)}, f32[1,1,128,256]{3,2,1,0:T(8,128)S(1)}, u32[]{:S(2)}, u32[]{:S(2)}) collective-permute-start(f32[1,1,128,256]{3,2,1,0:T(8,128)S(1)} %bitcast.346), channel_id=1, source_target_pairs={{8,0},{16,8},{24,16},{32,24},{40,32},{48,40},{56,48},{64,56},{72,6... | collective-permute-start | bytes 393224 | tf_op jit(solution)/shard_map/ppermute | solution.py:38
  250.0 2.5 collective-permute-start.11
  255.0 4.4 %collective-permute-done.10 = f32[1,1,128,256]{3,2,1,0:T(8,128)S(1)} collective-permute-done((f32[1,1,128,256]{3,2,1,0:T(8,128)S(1)}, f32[1,1,128,256]{3,2,1,0:T(8,128)S(1)}, u32[]{:S(2)}, u32[]{:S(2)}) %collective-permute-start.10) | collective-permute-done | bytes 131104 | tf_op jit(solution)/shard_map/ppermute | solution.py:38
  263.1 5.8 %collective-permute-start.16 = (f32[1,1,128,256]{3,2,1,0:T(8,128)S(1)}, f32[1,1,128,256]{3,2,1,0:T(8,128)S(1)}, u32[]{:S(2)}, u32[]{:S(2)}) collective-permute-start(f32[1,1,128,256]{3,2,1,0:T(8,128)S(1)} %bitcast.358), channel_id=1, source_target_pairs={{8,0},{16,8},{24,16},{32,24},{40,32},{48,40},{56,48},{64,56},{72,6... | collective-permute-start | bytes 393224 | tf_op jit(solution)/shard_map/ppermute | solution.py:38
  274.7 4.4 %collective-permute-done.14 = f32[1,1,128,256]{3,2,1,0:T(8,128)S(1)} collective-permute-done((f32[1,1,128,256]{3,2,1,0:T(8,128)S(1)}, f32[1,1,128,256]{3,2,1,0:T(8,128)S(1)}, u32[]{:S(2)}, u32[]{:S(2)}) %collective-permute-start.14) | collective-permute-done | bytes 131104 | tf_op jit(solution)/shard_map/ppermute | solution.py:38
  (156 shorter events, 85.0 us)
Async XLA Ops:
  0.6 88.6 %copy-start = (f32[256,256]{1,0:T(8,128)S(1)}, f32[256,256]{1,0:T(8,128)}, u32[]{:S(2)}) copy-start(f32[256,256]{1,0:T(8,128)} %param.7) | copy-start | bytes 786436
  0.6 6.2 %collective-permute-start.3 = (f32[1,1,128,256]{3,2,1,0:T(8,128)}, f32[1,1,128,256]{3,2,1,0:T(8,128)S(1)}, u32[]{:S(2)}, u32[]{:S(2)}) collective-permute-start(f32[1,1,128,256]{3,2,1,0:T(8,128)} %param.8), channel_id=1, source_target_pairs={{8,0},{16,8},{24,16},{32,24},{40,32},{48,40},{56,48},{64,56},{72,6... | collective-permute-start | bytes 393224 | tf_op jit(solution)/shard_map/ppermute | solution.py:52
  4.0 7.1 %collective-permute-start.2 = (f32[1,1,128,256]{3,2,1,0:T(8,128)}, f32[1,1,128,256]{3,2,1,0:T(8,128)S(1)}, u32[]{:S(2)}, u32[]{:S(2)}) collective-permute-start(f32[1,1,128,256]{3,2,1,0:T(8,128)} %param.8), channel_id=1, source_target_pairs={{1,0},{2,1},{3,2},{4,3},{5,4},{6,5},{7,6},{9,8},{10,9},{11,10},{12... | collective-permute-start | bytes 393224 | tf_op jit(solution)/shard_map/ppermute | solution.py:52
  31.5 57.7 %copy-start.5 = (f32[1,8,16,256]{3,2,1,0:T(8,128)S(1)}, f32[1,8,16,256]{3,2,1,0:T(8,128)}, u32[]{:S(2)}) copy-start(f32[1,8,16,256]{3,2,1,0:T(8,128)} %param.6) | copy-start | bytes 393220
  85.6 17.7 %all-to-all-start.5 = ((f32[8,192,128]{2,1,0:T(8,128)}), f32[8,192,128]{2,1,0:T(8,128)S(1)}, u32[]{:S(2)}, u32[]{:S(2)}) async-start(f32[8,192,128]{2,1,0:T(8,128)} %broadcast_in_dim.22), calls=%async_computation.5 | async-start | bytes 1572864 | tf_op jit(solution)/shard_map/all_to_all | solution.py:134
  89.5 8.5 %collective-permute-start.1 = (f32[1,8,16,256]{3,2,1,0:T(8,128)S(1)}, f32[1,8,16,256]{3,2,1,0:T(8,128)S(1)}, u32[]{:S(2)}, u32[]{:S(2)}) collective-permute-start(f32[1,8,16,256]{3,2,1,0:T(8,128)S(1)} %bitcast.342), channel_id=1, source_target_pairs={{0,8},{8,16},{16,24},{24,32},{32,40},{40,48},{48,56},{56,64},{64,7... | collective-permute-start | bytes 393224 | tf_op jit(solution)/shard_map/ppermute | solution.py:21
  91.8 8.2 %collective-permute-start = (f32[1,8,16,256]{3,2,1,0:T(8,128)S(1)}, f32[1,8,16,256]{3,2,1,0:T(8,128)S(1)}, u32[]{:S(2)}, u32[]{:S(2)}) collective-permute-start(f32[1,8,16,256]{3,2,1,0:T(8,128)S(1)} %bitcast.343), channel_id=1, source_target_pairs={{8,0},{16,8},{24,16},{32,24},{40,32},{48,40},{56,48},{64,56},{72,6... | collective-permute-start | bytes 393224 | tf_op jit(solution)/shard_map/ppermute | solution.py:24
  107.1 8.4 %collective-permute-start.5 = (f32[1,8,16,256]{3,2,1,0:T(8,128)S(1)}, f32[1,8,16,256]{3,2,1,0:T(8,128)S(1)}, u32[]{:S(2)}, u32[]{:S(2)}) collective-permute-start(f32[1,8,16,256]{3,2,1,0:T(8,128)S(1)} %bitcast.351), channel_id=1, source_target_pairs={{0,8},{8,16},{16,24},{24,32},{32,40},{40,48},{48,56},{56,64},{64,7... | collective-permute-start | bytes 393224 | tf_op jit(solution)/shard_map/ppermute | solution.py:21
  109.1 8.3 %collective-permute-start.4 = (f32[1,8,16,256]{3,2,1,0:T(8,128)S(1)}, f32[1,8,16,256]{3,2,1,0:T(8,128)S(1)}, u32[]{:S(2)}, u32[]{:S(2)}) collective-permute-start(f32[1,8,16,256]{3,2,1,0:T(8,128)S(1)} %bitcast.352), channel_id=1, source_target_pairs={{8,0},{16,8},{24,16},{32,24},{40,32},{48,40},{56,48},{64,56},{72,6... | collective-permute-start | bytes 393224 | tf_op jit(solution)/shard_map/ppermute | solution.py:24
  117.9 8.5 %collective-permute-start.7 = (f32[1,8,16,256]{3,2,1,0:T(8,128)S(1)}, f32[1,8,16,256]{3,2,1,0:T(8,128)S(1)}, u32[]{:S(2)}, u32[]{:S(2)}) collective-permute-start(f32[1,8,16,256]{3,2,1,0:T(8,128)S(1)} %bitcast.354), channel_id=1, source_target_pairs={{0,8},{8,16},{16,24},{24,32},{32,40},{40,48},{48,56},{56,64},{64,7... | collective-permute-start | bytes 393224 | tf_op jit(solution)/shard_map/ppermute | solution.py:21
  119.8 8.4 %collective-permute-start.6 = (f32[1,8,16,256]{3,2,1,0:T(8,128)S(1)}, f32[1,8,16,256]{3,2,1,0:T(8,128)S(1)}, u32[]{:S(2)}, u32[]{:S(2)}) collective-permute-start(f32[1,8,16,256]{3,2,1,0:T(8,128)S(1)} %bitcast.355), channel_id=1, source_target_pairs={{8,0},{16,8},{24,16},{32,24},{40,32},{48,40},{56,48},{64,56},{72,6... | collective-permute-start | bytes 393224 | tf_op jit(solution)/shard_map/ppermute | solution.py:24
  128.8 10.4 %copy-start.3 = (f32[8,16,256]{2,1,0:T(8,128)}, f32[8,16,256]{2,1,0:T(8,128)S(1)}, u32[]{:S(2)}) copy-start(f32[8,16,256]{2,1,0:T(8,128)S(1)} %fusion.32) | copy-start | bytes 393220
  128.8 10.2 %collective-permute-start.9 = (f32[1,8,16,256]{3,2,1,0:T(8,128)S(1)}, f32[1,8,16,256]{3,2,1,0:T(8,128)S(1)}, u32[]{:S(2)}, u32[]{:S(2)}) collective-permute-start(f32[1,8,16,256]{3,2,1,0:T(8,128)S(1)} %bitcast.364), channel_id=1, source_target_pairs={{0,8},{8,16},{16,24},{24,32},{32,40},{40,48},{48,56},{56,64},{64,7... | collective-permute-start | bytes 393224 | tf_op jit(solution)/shard_map/ppermute | solution.py:21
  130.7 8.4 %collective-permute-start.8 = (f32[1,8,16,256]{3,2,1,0:T(8,128)S(1)}, f32[1,8,16,256]{3,2,1,0:T(8,128)S(1)}, u32[]{:S(2)}, u32[]{:S(2)}) collective-permute-start(f32[1,8,16,256]{3,2,1,0:T(8,128)S(1)} %bitcast.365), channel_id=1, source_target_pairs={{8,0},{16,8},{24,16},{32,24},{40,32},{48,40},{56,48},{64,56},{72,6... | collective-permute-start | bytes 393224 | tf_op jit(solution)/shard_map/ppermute | solution.py:24
  192.3 19.4 %all-to-all-start.9 = ((f32[8,256,128]{2,1,0:T(8,128)}), f32[8,256,128]{2,1,0:T(8,128)S(1)}, u32[]{:S(2)}, u32[]{:S(2)}) async-start(f32[8,256,128]{2,1,0:T(8,128)} %broadcast_in_dim.26), calls=%async_computation.9 | async-start | bytes 2097152 | tf_op jit(solution)/shard_map/all_to_all | solution.py:134
  242.3 11.5 %collective-permute-start.13 = (f32[1,1,128,256]{3,2,1,0:T(8,128)S(1)}, f32[1,1,128,256]{3,2,1,0:T(8,128)S(1)}, u32[]{:S(2)}, u32[]{:S(2)}) collective-permute-start(f32[1,1,128,256]{3,2,1,0:T(8,128)S(1)} %bitcast.345), channel_id=1, source_target_pairs={{0,8},{8,16},{16,24},{24,32},{32,40},{40,48},{48,56},{56,64},{64,7... | collective-permute-start | bytes 393224 | tf_op jit(solution)/shard_map/ppermute | solution.py:37
  244.2 9.6 %collective-permute-start.12 = (f32[1,1,128,256]{3,2,1,0:T(8,128)S(1)}, f32[1,1,128,256]{3,2,1,0:T(8,128)S(1)}, u32[]{:S(2)}, u32[]{:S(2)}) collective-permute-start(f32[1,1,128,256]{3,2,1,0:T(8,128)S(1)} %bitcast.346), channel_id=1, source_target_pairs={{8,0},{16,8},{24,16},{32,24},{40,32},{48,40},{56,48},{64,56},{72,6... | collective-permute-start | bytes 393224 | tf_op jit(solution)/shard_map/ppermute | solution.py:38
  250.0 5.0 %collective-permute-start.11 = (f32[1,1,128,256]{3,2,1,0:T(8,128)S(1)}, f32[1,1,128,256]{3,2,1,0:T(8,128)S(1)}, u32[]{:S(2)}, u32[]{:S(2)}) collective-permute-start(f32[1,1,128,256]{3,2,1,0:T(8,128)S(1)} %bitcast.347), channel_id=1, source_target_pairs={{0,1},{1,2},{2,3},{3,4},{4,5},{5,6},{6,7},{8,9},{9,10},{10,11},{11... | collective-permute-start | bytes 393224 | tf_op jit(solution)/shard_map/ppermute | solution.py:37
  252.5 6.9 %collective-permute-start.10 = (f32[1,1,128,256]{3,2,1,0:T(8,128)S(1)}, f32[1,1,128,256]{3,2,1,0:T(8,128)S(1)}, u32[]{:S(2)}, u32[]{:S(2)}) collective-permute-start(f32[1,1,128,256]{3,2,1,0:T(8,128)S(1)} %bitcast.348), channel_id=1, source_target_pairs={{1,0},{2,1},{3,2},{4,3},{5,4},{6,5},{7,6},{9,8},{10,9},{11,10},{12... | collective-permute-start | bytes 393224 | tf_op jit(solution)/shard_map/ppermute | solution.py:38
  253.8 15.1 %copy-start.4 = (f32[8,16,256]{2,1,0:T(8,128)S(1)}, f32[8,16,256]{2,1,0:T(8,128)}, u32[]{:S(2)}) copy-start(f32[8,16,256]{2,1,0:T(8,128)} %copy-done.3) | copy-start | bytes 393220
  261.2 12.3 %collective-permute-start.17 = (f32[1,1,128,256]{3,2,1,0:T(8,128)S(1)}, f32[1,1,128,256]{3,2,1,0:T(8,128)S(1)}, u32[]{:S(2)}, u32[]{:S(2)}) collective-permute-start(f32[1,1,128,256]{3,2,1,0:T(8,128)S(1)} %bitcast.357), channel_id=1, source_target_pairs={{0,8},{8,16},{16,24},{24,32},{32,40},{40,48},{48,56},{56,64},{64,7... | collective-permute-start | bytes 393224 | tf_op jit(solution)/shard_map/ppermute | solution.py:37
  263.1 10.4 %collective-permute-start.16 = (f32[1,1,128,256]{3,2,1,0:T(8,128)S(1)}, f32[1,1,128,256]{3,2,1,0:T(8,128)S(1)}, u32[]{:S(2)}, u32[]{:S(2)}) collective-permute-start(f32[1,1,128,256]{3,2,1,0:T(8,128)S(1)} %bitcast.358), channel_id=1, source_target_pairs={{8,0},{16,8},{24,16},{32,24},{40,32},{48,40},{56,48},{64,56},{72,6... | collective-permute-start | bytes 393224 | tf_op jit(solution)/shard_map/ppermute | solution.py:38
  269.9 4.8 %collective-permute-start.15 = (f32[1,1,128,256]{3,2,1,0:T(8,128)S(1)}, f32[1,1,128,256]{3,2,1,0:T(8,128)S(1)}, u32[]{:S(2)}, u32[]{:S(2)}) collective-permute-start(f32[1,1,128,256]{3,2,1,0:T(8,128)S(1)} %bitcast.359), channel_id=1, source_target_pairs={{0,1},{1,2},{2,3},{3,4},{4,5},{5,6},{6,7},{8,9},{9,10},{10,11},{11... | collective-permute-start | bytes 393224 | tf_op jit(solution)/shard_map/ppermute | solution.py:37
  272.2 6.9 %collective-permute-start.14 = (f32[1,1,128,256]{3,2,1,0:T(8,128)S(1)}, f32[1,1,128,256]{3,2,1,0:T(8,128)S(1)}, u32[]{:S(2)}, u32[]{:S(2)}) collective-permute-start(f32[1,1,128,256]{3,2,1,0:T(8,128)S(1)} %bitcast.360), channel_id=1, source_target_pairs={{1,0},{2,1},{3,2},{4,3},{5,4},{6,5},{7,6},{9,8},{10,9},{11,10},{12... | collective-permute-start | bytes 393224 | tf_op jit(solution)/shard_map/ppermute | solution.py:38
  (3 other events, 7.2 us)

commit v4 on v1

--- a/solution.py
+++ b/solution.py
@@ -149,6 +149,20 @@
         lax.slice_in_dim(padded, 2, extent + 2, axis=which_dim)
         - lax.slice_in_dim(padded, 0, extent, axis=which_dim)
     )
+
+
+def final_first_moments(values, cells):
+    ahead = from_behind(values, GX, -1)
+    following = jnp.concatenate([values[1:], ahead], axis=0)
+    pairs = jnp.einsum("xyzr,xyzs->rs", values, following, precision=HIGHEST)
+    across = 0.5 * (pairs - pairs.T)
+    within = jnp.einsum(
+        "xyzr,dxyzs->drs",
+        values,
+        jnp.stack([central(values, 1), central(values, 2)]),
+        precision=HIGHEST,
+    )
+    return jnp.concatenate([across[None], within]) / cells
 
 
 def position_slopes(values):
@@ -280,12 +294,12 @@
     )
     raw_terms = jnp.stack(
         [
-            moments(final_section, position_slopes(final_section), pos_cells),
+            final_first_moments(final_section, pos_cells),
             moments(final_section, gravity[..., None] * final_section[None], pos_cells),
         ]
     )
     local_packed = jnp.concatenate([gram_part[None], raw_terms[0] + raw_terms[1]])
-    packed = staged_total(local_packed.reshape(-1), (("gx_1", "gx_2"), "gx_0")).reshape(
+    packed = staged_total(local_packed.reshape(-1), ("gx_2", ("gx_0", "gx_1"))).reshape(
         local_packed.shape
     )
     gram_matrix = 0.5 * (packed[0] + packed[0].T)

time: 274 us -> 268 us (0.978)
  blocking collectives: 135 us -> 129 us
    ppermute x4 -> x3, starting transfers between devices: 22.9 us -> 17 us  [padded_2(): lax.ppermute(lax.slice_in_dim(block, 0, width, axis=dim), axis, backward)]
    ppermute x2 -> x3, starting transfers between devices: 4.62 us -> 10.5 us  [from_behind(): return lax.ppermute(block, axis, route)]
    all_to_all x4, blocking collectives: 51.1 us -> 48 us  [staged_total(): part = lax.all_to_all(rows, axis, 0, 0, tiled=True).reshape(-1)]
    ppermute x4 -> x3, starting transfers between devices: 8.06 us -> 6.14 us  [padded_2(): lax.ppermute(lax.slice_in_dim(block, block.shape[dim] - width, None, axis...]
    ppermute x4 -> x3, waiting for transfers between devices: 5.7 us -> 5.62 us  [padded_2(): lax.ppermute(lax.slice_in_dim(block, 0, width, axis=dim), axis, backward)]
  transfers between devices with their start and end apart: 19 -> 18, of which waited for: 13 -> 13; matrix products, arithmetic and copies ran while one was open for 3% -> 3% of each run, Pallas kernels for 0% -> 0%
where the time goes in v4:
time: 268 us; the launch traced here: 266 us
  blocking collectives  129 us (48%)
  starting transfers between devices  59.9 us (22%)
  matrix products  33.7 us (13%)
  waiting for transfers between devices  24.6 us (9%)
  local copies, waits for them, and re-layouts  11.6 us (4%)
  other arithmetic  5.33 us (2%)
    all_to_all x5, blocking collectives, staged_total(): lax.all_to_all(rows, axis, 0, 0, tiled=True)  81 us
    all_to_all x4, blocking collectives, staged_total(): part = lax.all_to_all(rows, axis, 0, 0, tiled=True).reshape(-1)  48 us
    ppermute x3, starting transfers between devices, padded_2(): lax.ppermute(lax.slice_in_dim(block, 0, width, axis=dim), axis, backward)  17 us
    ppermute x4, starting transfers between devices, extended(): lax.ppermute(first, axis, [(b, a) for a, b in up])  14 us
    ppermute x3, starting transfers between devices, from_behind(): return lax.ppermute(block, axis, route)  10.5 us
    ppermute x4, starting transfers between devices, extended(): lax.ppermute(last, axis, up)  8.76 us
    ppermute x4, waiting for transfers between devices, extended(): lax.ppermute(first, axis, [(b, a) for a, b in up])  8.73 us
    ppermute x3, starting transfers between devices, padded_2(): lax.ppermute(lax.slice_in_dim(block, block.shape[dim] - width, None, axis...  6.14 us
  transfers between devices with their start and end apart: 18, of which 13 were waited for; matrix products, arithmetic and copies ran while one was open for 3% of the time, Pallas kernels for 0%

profile of v4, /device:TPU:64, one launch (start us, length us, event | category | flops | bytes accessed | tf_op | source)
XLA Modules:
  0.0 266.5 jit_solution(2906540264235809634)
XLA Ops:
  0.6 3.3 %collective-permute-start.3 = (f32[1,1,128,256]{3,2,1,0:T(8,128)}, f32[1,1,128,256]{3,2,1,0:T(8,128)S(1)}, u32[]{:S(2)}, u32[]{:S(2)}) collective-permute-start(f32[1,1,128,256]{3,2,1,0:T(8,128)} %param.6), channel_id=1, source_target_pairs={{8,0},{16,8},{24,16},{32,24},{40,32},{48,40},{56,48},{64,56},{72,6... | collective-permute-start | bytes 393224 | tf_op jit(solution)/shard_map/ppermute | solution.py:52
  8.2 2.9 %collective-permute-done.2 = f32[1,1,128,256]{3,2,1,0:T(8,128)S(1)} collective-permute-done((f32[1,1,128,256]{3,2,1,0:T(8,128)}, f32[1,1,128,256]{3,2,1,0:T(8,128)S(1)}, u32[]{:S(2)}, u32[]{:S(2)}) %collective-permute-start.2) | collective-permute-done | bytes 131104 | tf_op jit(solution)/shard_map/ppermute | solution.py:52
  14.5 16.9 %all_to_all.50 = f32[8,192,128]{2,1,0:T(8,128)S(1)} all-to-all(f32[8,192,128]{2,1,0:T(8,128)S(1)} %reshape.203), channel_id=1, replica_groups=mesh['gx_0'=8,'gx_1'=4,'gx_2'=2,'vert'=8] {'gx_1','gx_2'}, dimensions={0} | all-to-all | bytes 1572864 | tf_op jit(solution)/shard_map/all_to_all | solution.py:131
  31.5 15.8 %all_to_all.51 = f32[8,24,128]{2,1,0:T(8,128)S(1)} all-to-all(f32[8,24,128]{2,1,0:T(8,128)S(1)} %bitcast.416), channel_id=1, replica_groups=mesh['gx_0'=8,'gx_1'=4,'gx_2'=2,'vert'=8] {'vert'}, dimensions={0} | all-to-all | bytes 196608 | tf_op jit(solution)/shard_map/all_to_all | solution.py:131
  47.3 16.1 %all_to_all.52 = f32[8,3,128]{2,1,0:T(4,128)S(1)} all-to-all(f32[8,3,128]{2,1,0:T(4,128)S(1)} %reshape_reshape.21), channel_id=1, replica_groups=mesh['gx_0'=8,'gx_1'=4,'gx_2'=2,'vert'=8] {'gx_0'}, dimensions={0} | all-to-all | bytes 24576 | tf_op jit(solution)/shard_map/all_to_all | solution.py:131
  63.4 10.1 %all_to_all.53 = f32[8,3,128]{2,1,0:T(4,128)S(1)} all-to-all(f32[8,3,128]{2,1,0:T(4,128)S(1)} %broadcast_in_dim.20), channel_id=1, replica_groups=mesh['gx_0'=8,'gx_1'=4,'gx_2'=2,'vert'=8] {'gx_0'}, dimensions={0} | all-to-all | bytes 24576 | tf_op jit(solution)/shard_map/all_to_all | solution.py:134
  73.6 11.1 %all_to_all.54 = f32[8,24,128]{2,1,0:T(8,128)S(1)} all-to-all(f32[8,24,128]{2,1,0:T(8,128)S(1)} %broadcast_in_dim.22), channel_id=1, replica_groups=mesh['gx_0'=8,'gx_1'=4,'gx_2'=2,'vert'=8] {'vert'}, dimensions={0} | all-to-all | bytes 196608 | tf_op jit(solution)/shard_map/all_to_all | solution.py:134
  85.7 3.5 %all-to-all-start.5 = ((f32[8,192,128]{2,1,0:T(8,128)}), f32[8,192,128]{2,1,0:T(8,128)S(1)}, u32[]{:S(2)}, u32[]{:S(2)}) async-start(f32[8,192,128]{2,1,0:T(8,128)} %broadcast_in_dim.24), calls=%async_computation.5 | async-start | bytes 1572864 | tf_op jit(solution)/shard_map/all_to_all | solution.py:134
  91.8 5.4 %collective-permute-start = (f32[1,8,16,256]{3,2,1,0:T(8,128)S(1)}, f32[1,8,16,256]{3,2,1,0:T(8,128)S(1)}, u32[]{:S(2)}, u32[]{:S(2)}) collective-permute-start(f32[1,8,16,256]{3,2,1,0:T(8,128)S(1)} %bitcast.393), channel_id=1, source_target_pairs={{8,0},{16,8},{24,16},{32,24},{40,32},{48,40},{56,48},{64,56},{72,6... | collective-permute-start | bytes 393224 | tf_op jit(solution)/shard_map/ppermute | solution.py:24
  100.1 3.3 %all-to-all-done.5 = f32[8,192,128]{2,1,0:T(8,128)S(1)} async-done(((f32[8,192,128]{2,1,0:T(8,128)}), f32[8,192,128]{2,1,0:T(8,128)S(1)}, u32[]{:S(2)}, u32[]{:S(2)}) %all-to-all-start.5) | async-done | bytes 786464 | tf_op jit(solution)/shard_map/all_to_all | solution.py:134
  109.1 5.8 %collective-permute-start.4 = (f32[1,8,16,256]{3,2,1,0:T(8,128)S(1)}, f32[1,8,16,256]{3,2,1,0:T(8,128)S(1)}, u32[]{:S(2)}, u32[]{:S(2)}) collective-permute-start(f32[1,8,16,256]{3,2,1,0:T(8,128)S(1)} %bitcast.404), channel_id=1, source_target_pairs={{8,0},{16,8},{24,16},{32,24},{40,32},{48,40},{56,48},{64,56},{72,6... | collective-permute-start | bytes 393224 | tf_op jit(solution)/shard_map/ppermute | solution.py:24
  119.8 5.9 %collective-permute-start.6 = (f32[1,8,16,256]{3,2,1,0:T(8,128)S(1)}, f32[1,8,16,256]{3,2,1,0:T(8,128)S(1)}, u32[]{:S(2)}, u32[]{:S(2)}) collective-permute-start(f32[1,8,16,256]{3,2,1,0:T(8,128)S(1)} %bitcast.407), channel_id=1, source_target_pairs={{8,0},{16,8},{24,16},{32,24},{40,32},{48,40},{56,48},{64,56},{72,6... | collective-permute-start | bytes 393224 | tf_op jit(solution)/shard_map/ppermute | solution.py:24
  129.2 5.9 %collective-permute-start.8 = (f32[1,8,16,256]{3,2,1,0:T(8,128)S(1)}, f32[1,8,16,256]{3,2,1,0:T(8,128)S(1)}, u32[]{:S(2)}, u32[]{:S(2)}) collective-permute-start(f32[1,8,16,256]{3,2,1,0:T(8,128)S(1)} %bitcast.414), channel_id=1, source_target_pairs={{8,0},{16,8},{24,16},{32,24},{40,32},{48,40},{56,48},{64,56},{72,6... | collective-permute-start | bytes 393224 | tf_op jit(solution)/shard_map/ppermute | solution.py:52
  143.0 5.4 %all_to_all.55 = f32[2,1024,128]{2,1,0:T(8,128)} all-to-all(f32[2,1024,128]{2,1,0:T(8,128)S(1)} %reshape.208), channel_id=1, replica_groups=mesh['gx_0'=8,'gx_1'=4,'gx_2'=2,'vert'=8] {'gx_2'}, dimensions={0} | all-to-all | bytes 2097152 | tf_op jit(solution)/shard_map/all_to_all | solution.py:131
  149.7 26.8 %all_to_all.56 = f32[32,32,128]{2,1,0:T(8,128)S(1)} all-to-all(f32[32,32,128]{2,1,0:T(8,128)S(1)} %bitcast.402), channel_id=1, replica_groups=mesh['gx_0'=8,'gx_1'=4,'gx_2'=2,'vert'=8] {'gx_0','gx_1'}, dimensions={0} | all-to-all | bytes 1048576 | tf_op jit(solution)/shard_map/all_to_all | solution.py:131
  176.6 21.4 %all_to_all.57 = f32[32,32,128]{2,1,0:T(8,128)S(1)} all-to-all(f32[32,32,128]{2,1,0:T(8,128)S(1)} %broadcast_in_dim.27), channel_id=1, replica_groups=mesh['gx_0'=8,'gx_1'=4,'gx_2'=2,'vert'=8] {'gx_0','gx_1'}, dimensions={0} | all-to-all | bytes 1048576 | tf_op jit(solution)/shard_map/all_to_all | solution.py:134
  198.1 5.4 %all_to_all.58 = f32[2,1024,128]{2,1,0:T(8,128)} all-to-all(f32[2,1024,128]{2,1,0:T(8,128)S(1)} %broadcast_in_dim.29), channel_id=1, replica_groups=mesh['gx_0'=8,'gx_1'=4,'gx_2'=2,'vert'=8] {'gx_2'}, dimensions={0} | all-to-all | bytes 2097152 | tf_op jit(solution)/shard_map/all_to_all | solution.py:134
  216.7 2.3 copy.101
  229.2 5.6 %collective-permute-start.11 = (f32[1,1,128,256]{3,2,1,0:T(8,128)S(1)}, f32[1,1,128,256]{3,2,1,0:T(8,128)S(1)}, u32[]{:S(2)}, u32[]{:S(2)}) collective-permute-start(f32[1,1,128,256]{3,2,1,0:T(8,128)S(1)} %bitcast.397), channel_id=1, source_target_pairs={{8,0},{16,8},{24,16},{32,24},{40,32},{48,40},{56,48},{64,56},{72,6... | collective-permute-start | bytes 393224 | tf_op jit(solution)/shard_map/ppermute | solution.py:38
  234.9 2.5 collective-permute-start.10
  239.9 4.4 %collective-permute-done.9 = f32[1,1,128,256]{3,2,1,0:T(8,128)S(1)} collective-permute-done((f32[1,1,128,256]{3,2,1,0:T(8,128)S(1)}, f32[1,1,128,256]{3,2,1,0:T(8,128)S(1)}, u32[]{:S(2)}, u32[]{:S(2)}) %collective-permute-start.9) | collective-permute-done | bytes 131104 | tf_op jit(solution)/shard_map/ppermute | solution.py:38
  248.0 5.8 %collective-permute-start.15 = (f32[1,1,128,256]{3,2,1,0:T(8,128)S(1)}, f32[1,1,128,256]{3,2,1,0:T(8,128)S(1)}, u32[]{:S(2)}, u32[]{:S(2)}) collective-permute-start(f32[1,1,128,256]{3,2,1,0:T(8,128)S(1)} %bitcast.410), channel_id=1, source_target_pairs={{8,0},{16,8},{24,16},{32,24},{40,32},{48,40},{56,48},{64,56},{72,6... | collective-permute-start | bytes 393224 | tf_op jit(solution)/shard_map/ppermute | solution.py:38
  254.7 2.3 collective-permute-start.14
  259.6 4.4 %collective-permute-done.13 = f32[1,1,128,256]{3,2,1,0:T(8,128)S(1)} collective-permute-done((f32[1,1,128,256]{3,2,1,0:T(8,128)S(1)}, f32[1,1,128,256]{3,2,1,0:T(8,128)S(1)}, u32[]{:S(2)}, u32[]{:S(2)}) %collective-permute-start.13) | collective-permute-done | bytes 131104 | tf_op jit(solution)/shard_map/ppermute | solution.py:38
  (133 shorter events, 72.0 us)
Async XLA Ops:
  0.6 88.6 %copy-start = (f32[256,256]{1,0:T(8,128)S(1)}, f32[256,256]{1,0:T(8,128)}, u32[]{:S(2)}) copy-start(f32[256,256]{1,0:T(8,128)} %param.5) | copy-start | bytes 786436
  0.6 6.2 %collective-permute-start.3 = (f32[1,1,128,256]{3,2,1,0:T(8,128)}, f32[1,1,128,256]{3,2,1,0:T(8,128)S(1)}, u32[]{:S(2)}, u32[]{:S(2)}) collective-permute-start(f32[1,1,128,256]{3,2,1,0:T(8,128)} %param.6), channel_id=1, source_target_pairs={{8,0},{16,8},{24,16},{32,24},{40,32},{48,40},{56,48},{64,56},{72,6... | collective-permute-start | bytes 393224 | tf_op jit(solution)/shard_map/ppermute | solution.py:52
  4.0 7.1 %collective-permute-start.2 = (f32[1,1,128,256]{3,2,1,0:T(8,128)}, f32[1,1,128,256]{3,2,1,0:T(8,128)S(1)}, u32[]{:S(2)}, u32[]{:S(2)}) collective-permute-start(f32[1,1,128,256]{3,2,1,0:T(8,128)} %param.6), channel_id=1, source_target_pairs={{1,0},{2,1},{3,2},{4,3},{5,4},{6,5},{7,6},{9,8},{10,9},{11,10},{12... | collective-permute-start | bytes 393224 | tf_op jit(solution)/shard_map/ppermute | solution.py:52
  12.4 0.9 copy-start.1
  31.5 57.7 %copy-start.4 = (f32[1,8,16,256]{3,2,1,0:T(8,128)S(1)}, f32[1,8,16,256]{3,2,1,0:T(8,128)}, u32[]{:S(2)}) copy-start(f32[1,8,16,256]{3,2,1,0:T(8,128)} %param.4) | copy-start | bytes 393220
  85.7 17.7 %all-to-all-start.5 = ((f32[8,192,128]{2,1,0:T(8,128)}), f32[8,192,128]{2,1,0:T(8,128)S(1)}, u32[]{:S(2)}, u32[]{:S(2)}) async-start(f32[8,192,128]{2,1,0:T(8,128)} %broadcast_in_dim.24), calls=%async_computation.5 | async-start | bytes 1572864 | tf_op jit(solution)/shard_map/all_to_all | solution.py:134
  89.5 8.5 %collective-permute-start.1 = (f32[1,8,16,256]{3,2,1,0:T(8,128)S(1)}, f32[1,8,16,256]{3,2,1,0:T(8,128)S(1)}, u32[]{:S(2)}, u32[]{:S(2)}) collective-permute-start(f32[1,8,16,256]{3,2,1,0:T(8,128)S(1)} %bitcast.392), channel_id=1, source_target_pairs={{0,8},{8,16},{16,24},{24,32},{32,40},{40,48},{48,56},{56,64},{64,7... | collective-permute-start | bytes 393224 | tf_op jit(solution)/shard_map/ppermute | solution.py:21
  91.8 8.2 %collective-permute-start = (f32[1,8,16,256]{3,2,1,0:T(8,128)S(1)}, f32[1,8,16,256]{3,2,1,0:T(8,128)S(1)}, u32[]{:S(2)}, u32[]{:S(2)}) collective-permute-start(f32[1,8,16,256]{3,2,1,0:T(8,128)S(1)} %bitcast.393), channel_id=1, source_target_pairs={{8,0},{16,8},{24,16},{32,24},{40,32},{48,40},{56,48},{64,56},{72,6... | collective-permute-start | bytes 393224 | tf_op jit(solution)/shard_map/ppermute | solution.py:24
  104.8 1.3 copy-start.5
  107.2 8.4 %collective-permute-start.5 = (f32[1,8,16,256]{3,2,1,0:T(8,128)S(1)}, f32[1,8,16,256]{3,2,1,0:T(8,128)S(1)}, u32[]{:S(2)}, u32[]{:S(2)}) collective-permute-start(f32[1,8,16,256]{3,2,1,0:T(8,128)S(1)} %bitcast.403), channel_id=1, source_target_pairs={{0,8},{8,16},{16,24},{24,32},{32,40},{40,48},{48,56},{56,64},{64,7... | collective-permute-start | bytes 393224 | tf_op jit(solution)/shard_map/ppermute | solution.py:21
  109.1 8.3 %collective-permute-start.4 = (f32[1,8,16,256]{3,2,1,0:T(8,128)S(1)}, f32[1,8,16,256]{3,2,1,0:T(8,128)S(1)}, u32[]{:S(2)}, u32[]{:S(2)}) collective-permute-start(f32[1,8,16,256]{3,2,1,0:T(8,128)S(1)} %bitcast.404), channel_id=1, source_target_pairs={{8,0},{16,8},{24,16},{32,24},{40,32},{48,40},{56,48},{64,56},{72,6... | collective-permute-start | bytes 393224 | tf_op jit(solution)/shard_map/ppermute | solution.py:24
  117.9 8.5 %collective-permute-start.7 = (f32[1,8,16,256]{3,2,1,0:T(8,128)S(1)}, f32[1,8,16,256]{3,2,1,0:T(8,128)S(1)}, u32[]{:S(2)}, u32[]{:S(2)}) collective-permute-start(f32[1,8,16,256]{3,2,1,0:T(8,128)S(1)} %bitcast.406), channel_id=1, source_target_pairs={{0,8},{8,16},{16,24},{24,32},{32,40},{40,48},{48,56},{56,64},{64,7... | collective-permute-start | bytes 393224 | tf_op jit(solution)/shard_map/ppermute | solution.py:21
  119.8 8.4 %collective-permute-start.6 = (f32[1,8,16,256]{3,2,1,0:T(8,128)S(1)}, f32[1,8,16,256]{3,2,1,0:T(8,128)S(1)}, u32[]{:S(2)}, u32[]{:S(2)}) collective-permute-start(f32[1,8,16,256]{3,2,1,0:T(8,128)S(1)} %bitcast.407), channel_id=1, source_target_pairs={{8,0},{16,8},{24,16},{32,24},{40,32},{48,40},{56,48},{64,56},{72,6... | collective-permute-start | bytes 393224 | tf_op jit(solution)/shard_map/ppermute | solution.py:24
  128.8 9.6 %copy-start.2 = (f32[8,16,256]{2,1,0:T(8,128)}, f32[8,16,256]{2,1,0:T(8,128)S(1)}, u32[]{:S(2)}) copy-start(f32[8,16,256]{2,1,0:T(8,128)S(1)} %fusion.36) | copy-start | bytes 393220
  129.2 8.4 %collective-permute-start.8 = (f32[1,8,16,256]{3,2,1,0:T(8,128)S(1)}, f32[1,8,16,256]{3,2,1,0:T(8,128)S(1)}, u32[]{:S(2)}, u32[]{:S(2)}) collective-permute-start(f32[1,8,16,256]{3,2,1,0:T(8,128)S(1)} %bitcast.414), channel_id=1, source_target_pairs={{8,0},{16,8},{24,16},{32,24},{40,32},{48,40},{56,48},{64,56},{72,6... | collective-permute-start | bytes 393224 | tf_op jit(solution)/shard_map/ppermute | solution.py:52
  227.2 11.5 %collective-permute-start.12 = (f32[1,1,128,256]{3,2,1,0:T(8,128)S(1)}, f32[1,1,128,256]{3,2,1,0:T(8,128)S(1)}, u32[]{:S(2)}, u32[]{:S(2)}) collective-permute-start(f32[1,1,128,256]{3,2,1,0:T(8,128)S(1)} %bitcast.396), channel_id=1, source_target_pairs={{0,8},{8,16},{16,24},{24,32},{32,40},{40,48},{48,56},{56,64},{64,7... | collective-permute-start | bytes 393224 | tf_op jit(solution)/shard_map/ppermute | solution.py:37
  229.2 9.5 %collective-permute-start.11 = (f32[1,1,128,256]{3,2,1,0:T(8,128)S(1)}, f32[1,1,128,256]{3,2,1,0:T(8,128)S(1)}, u32[]{:S(2)}, u32[]{:S(2)}) collective-permute-start(f32[1,1,128,256]{3,2,1,0:T(8,128)S(1)} %bitcast.397), channel_id=1, source_target_pairs={{8,0},{16,8},{24,16},{32,24},{40,32},{48,40},{56,48},{64,56},{72,6... | collective-permute-start | bytes 393224 | tf_op jit(solution)/shard_map/ppermute | solution.py:38
  234.9 5.0 %collective-permute-start.10 = (f32[1,1,128,256]{3,2,1,0:T(8,128)S(1)}, f32[1,1,128,256]{3,2,1,0:T(8,128)S(1)}, u32[]{:S(2)}, u32[]{:S(2)}) collective-permute-start(f32[1,1,128,256]{3,2,1,0:T(8,128)S(1)} %bitcast.398), channel_id=1, source_target_pairs={{0,1},{1,2},{2,3},{3,4},{4,5},{5,6},{6,7},{8,9},{9,10},{10,11},{11... | collective-permute-start | bytes 393224 | tf_op jit(solution)/shard_map/ppermute | solution.py:37
  237.4 6.9 %collective-permute-start.9 = (f32[1,1,128,256]{3,2,1,0:T(8,128)S(1)}, f32[1,1,128,256]{3,2,1,0:T(8,128)S(1)}, u32[]{:S(2)}, u32[]{:S(2)}) collective-permute-start(f32[1,1,128,256]{3,2,1,0:T(8,128)S(1)} %bitcast.399), channel_id=1, source_target_pairs={{1,0},{2,1},{3,2},{4,3},{5,4},{6,5},{7,6},{9,8},{10,9},{11,10},{12... | collective-permute-start | bytes 393224 | tf_op jit(solution)/shard_map/ppermute | solution.py:38
  238.7 15.1 %copy-start.3 = (f32[8,16,256]{2,1,0:T(8,128)S(1)}, f32[8,16,256]{2,1,0:T(8,128)}, u32[]{:S(2)}) copy-start(f32[8,16,256]{2,1,0:T(8,128)} %copy-done.2) | copy-start | bytes 393220
  246.1 12.3 %collective-permute-start.16 = (f32[1,1,128,256]{3,2,1,0:T(8,128)S(1)}, f32[1,1,128,256]{3,2,1,0:T(8,128)S(1)}, u32[]{:S(2)}, u32[]{:S(2)}) collective-permute-start(f32[1,1,128,256]{3,2,1,0:T(8,128)S(1)} %bitcast.409), channel_id=1, source_target_pairs={{0,8},{8,16},{16,24},{24,32},{32,40},{40,48},{48,56},{56,64},{64,7... | collective-permute-start | bytes 393224 | tf_op jit(solution)/shard_map/ppermute | solution.py:37
  248.0 10.4 %collective-permute-start.15 = (f32[1,1,128,256]{3,2,1,0:T(8,128)S(1)}, f32[1,1,128,256]{3,2,1,0:T(8,128)S(1)}, u32[]{:S(2)}, u32[]{:S(2)}) collective-permute-start(f32[1,1,128,256]{3,2,1,0:T(8,128)S(1)} %bitcast.410), channel_id=1, source_target_pairs={{8,0},{16,8},{24,16},{32,24},{40,32},{48,40},{56,48},{64,56},{72,6... | collective-permute-start | bytes 393224 | tf_op jit(solution)/shard_map/ppermute | solution.py:38
  254.7 4.8 %collective-permute-start.14 = (f32[1,1,128,256]{3,2,1,0:T(8,128)S(1)}, f32[1,1,128,256]{3,2,1,0:T(8,128)S(1)}, u32[]{:S(2)}, u32[]{:S(2)}) collective-permute-start(f32[1,1,128,256]{3,2,1,0:T(8,128)S(1)} %bitcast.411), channel_id=1, source_target_pairs={{0,1},{1,2},{2,3},{3,4},{4,5},{5,6},{6,7},{8,9},{9,10},{10,11},{11... | collective-permute-start | bytes 393224 | tf_op jit(solution)/shard_map/ppermute | solution.py:37
  257.1 6.9 %collective-permute-start.13 = (f32[1,1,128,256]{3,2,1,0:T(8,128)S(1)}, f32[1,1,128,256]{3,2,1,0:T(8,128)S(1)}, u32[]{:S(2)}, u32[]{:S(2)}) collective-permute-start(f32[1,1,128,256]{3,2,1,0:T(8,128)S(1)} %bitcast.412), channel_id=1, source_target_pairs={{1,0},{2,1},{3,2},{4,3},{5,4},{6,5},{7,6},{9,8},{10,9},{11,10},{12... | collective-permute-start | bytes 393224 | tf_op jit(solution)/shard_map/ppermute | solution.py:38

commit v5 on v4

--- a/solution.py
+++ b/solution.py
@@ -275,7 +275,7 @@
     vel_second = 0.5 * (pair_sums - jnp.swapaxes(pair_sums, 1, 2)) / vel_cells
     vel_packed = (vel_first + vel_second).reshape(-1)
     vel_mats = split_parts(
-        staged_total(vel_packed, (("gx_1", "gx_2"), "vert", "gx_0")).reshape(vel_first.shape)
+        staged_total(vel_packed, (("gx_1", "gx_2"), ("gx_0", "vert"))).reshape(vel_first.shape)
     )
 
     def position_rate(values):

time: 268 us -> 259 us (0.966)
  blocking collectives: 129 us -> 120 us
    all_to_all x4 -> x3, blocking collectives: 48 us -> 43.5 us  [staged_total(): part = lax.all_to_all(rows, axis, 0, 0, tiled=True).reshape(-1)]
    all_to_all x5 -> x4, blocking collectives: 81 us -> 76.9 us  [staged_total(): lax.all_to_all(rows, axis, 0, 0, tiled=True)]
where the time goes in v5:
time: 259 us; the launch traced here: 258 us
  blocking collectives  120 us (46%)
  starting transfers between devices  60.1 us (23%)
  matrix products  33.7 us (13%)
  waiting for transfers between devices  24.4 us (9%)
  local copies, waits for them, and re-layouts  11.7 us (5%)
  other arithmetic  5.37 us (2%)
    all_to_all x4, blocking collectives, staged_total(): lax.all_to_all(rows, axis, 0, 0, tiled=True)  76.9 us
    all_to_all x3, blocking collectives, staged_total(): part = lax.all_to_all(rows, axis, 0, 0, tiled=True).reshape(-1)  43.5 us
    ppermute x3, starting transfers between devices, padded_2(): lax.ppermute(lax.slice_in_dim(block, 0, width, axis=dim), axis, backward)  17 us
    ppermute x4, starting transfers between devices, extended(): lax.ppermute(first, axis, [(b, a) for a, b in up])  14 us
    ppermute x3, starting transfers between devices, from_behind(): return lax.ppermute(block, axis, route)  10.7 us
    ppermute x4, starting transfers between devices, extended(): lax.ppermute(last, axis, up)  8.74 us
    ppermute x4, waiting for transfers between devices, extended(): lax.ppermute(first, axis, [(b, a) for a, b in up])  8.73 us
    ppermute x3, starting transfers between devices, padded_2(): lax.ppermute(lax.slice_in_dim(block, block.shape[dim] - width, None, axis...  6.14 us
  transfers between devices with their start and end apart: 18, of which 13 were waited for; matrix products, arithmetic and copies ran while one was open for 3% of the time, Pallas kernels for 0%

profile of v5, /device:TPU:64, one launch (start us, length us, event | category | flops | bytes accessed | tf_op | source)
XLA Modules:
  0.0 258.0 jit_solution(16896167164585513197)
XLA Ops:
  0.6 3.3 %collective-permute-start.3 = (f32[1,1,128,256]{3,2,1,0:T(8,128)}, f32[1,1,128,256]{3,2,1,0:T(8,128)S(1)}, u32[]{:S(2)}, u32[]{:S(2)}) collective-permute-start(f32[1,1,128,256]{3,2,1,0:T(8,128)} %param.6), channel_id=1, source_target_pairs={{8,0},{16,8},{24,16},{32,24},{40,32},{48,40},{56,48},{64,56},{72,6... | collective-permute-start | bytes 393224 | tf_op jit(solution)/shard_map/ppermute | solution.py:52
  8.2 2.9 %collective-permute-done.2 = f32[1,1,128,256]{3,2,1,0:T(8,128)S(1)} collective-permute-done((f32[1,1,128,256]{3,2,1,0:T(8,128)}, f32[1,1,128,256]{3,2,1,0:T(8,128)S(1)}, u32[]{:S(2)}, u32[]{:S(2)}) %collective-permute-start.2) | collective-permute-done | bytes 131104 | tf_op jit(solution)/shard_map/ppermute | solution.py:52
  14.5 16.9 %all_to_all.40 = f32[8,192,128]{2,1,0:T(8,128)S(1)} all-to-all(f32[8,192,128]{2,1,0:T(8,128)S(1)} %reshape.202), channel_id=1, replica_groups=mesh['gx_0'=8,'gx_1'=4,'gx_2'=2,'vert'=8] {'gx_1','gx_2'}, dimensions={0} | all-to-all | bytes 1572864 | tf_op jit(solution)/shard_map/all_to_all | solution.py:131
  31.5 27.4 %all_to_all.41 = f32[64,3,128]{2,1,0:T(4,128)S(1)} all-to-all(f32[64,3,128]{2,1,0:T(4,128)S(1)} %reshape_reshape.16), channel_id=1, replica_groups=mesh['gx_0'=8,'gx_1'=4,'gx_2'=2,'vert'=8] {'gx_0','vert'}, dimensions={0} | all-to-all | bytes 196608 | tf_op jit(solution)/shard_map/all_to_all | solution.py:131
  59.0 16.7 %all_to_all.42 = f32[64,3,128]{2,1,0:T(4,128)S(1)} all-to-all(f32[64,3,128]{2,1,0:T(4,128)S(1)} %broadcast_in_dim.16), channel_id=1, replica_groups=mesh['gx_0'=8,'gx_1'=4,'gx_2'=2,'vert'=8] {'gx_0','vert'}, dimensions={0} | all-to-all | bytes 196608 | tf_op jit(solution)/shard_map/all_to_all | solution.py:134
  76.7 3.5 %all-to-all-start.3 = ((f32[8,192,128]{2,1,0:T(8,128)}), f32[8,192,128]{2,1,0:T(8,128)S(1)}, u32[]{:S(2)}, u32[]{:S(2)}) async-start(f32[8,192,128]{2,1,0:T(8,128)} %broadcast_in_dim.18), calls=%async_computation.3 | async-start | bytes 1572864 | tf_op jit(solution)/shard_map/all_to_all | solution.py:134
  80.6 2.3 collective-permute-start.1
  82.9 5.4 %collective-permute-start = (f32[1,8,16,256]{3,2,1,0:T(8,128)S(1)}, f32[1,8,16,256]{3,2,1,0:T(8,128)S(1)}, u32[]{:S(2)}, u32[]{:S(2)}) collective-permute-start(f32[1,8,16,256]{3,2,1,0:T(8,128)S(1)} %bitcast.391), channel_id=1, source_target_pairs={{8,0},{16,8},{24,16},{32,24},{40,32},{48,40},{56,48},{64,56},{72,6... | collective-permute-start | bytes 393224 | tf_op jit(solution)/shard_map/ppermute | solution.py:24
  89.1 2.0 collective-permute-done
  91.1 3.3 %all-to-all-done.3 = f32[8,192,128]{2,1,0:T(8,128)S(1)} async-done(((f32[8,192,128]{2,1,0:T(8,128)}), f32[8,192,128]{2,1,0:T(8,128)S(1)}, u32[]{:S(2)}, u32[]{:S(2)}) %all-to-all-start.3) | async-done | bytes 786464 | tf_op jit(solution)/shard_map/all_to_all | solution.py:134
  100.1 5.8 %collective-permute-start.4 = (f32[1,8,16,256]{3,2,1,0:T(8,128)S(1)}, f32[1,8,16,256]{3,2,1,0:T(8,128)S(1)}, u32[]{:S(2)}, u32[]{:S(2)}) collective-permute-start(f32[1,8,16,256]{3,2,1,0:T(8,128)S(1)} %bitcast.402), channel_id=1, source_target_pairs={{8,0},{16,8},{24,16},{32,24},{40,32},{48,40},{56,48},{64,56},{72,6... | collective-permute-start | bytes 393224 | tf_op jit(solution)/shard_map/ppermute | solution.py:24
  110.9 5.9 %collective-permute-start.6 = (f32[1,8,16,256]{3,2,1,0:T(8,128)S(1)}, f32[1,8,16,256]{3,2,1,0:T(8,128)S(1)}, u32[]{:S(2)}, u32[]{:S(2)}) collective-permute-start(f32[1,8,16,256]{3,2,1,0:T(8,128)S(1)} %bitcast.405), channel_id=1, source_target_pairs={{8,0},{16,8},{24,16},{32,24},{40,32},{48,40},{56,48},{64,56},{72,6... | collective-permute-start | bytes 393224 | tf_op jit(solution)/shard_map/ppermute | solution.py:24
  120.3 6.1 %collective-permute-start.8 = (f32[1,8,16,256]{3,2,1,0:T(8,128)S(1)}, f32[1,8,16,256]{3,2,1,0:T(8,128)S(1)}, u32[]{:S(2)}, u32[]{:S(2)}) collective-permute-start(f32[1,8,16,256]{3,2,1,0:T(8,128)S(1)} %bitcast.412), channel_id=1, source_target_pairs={{8,0},{16,8},{24,16},{32,24},{40,32},{48,40},{56,48},{64,56},{72,6... | collective-permute-start | bytes 393224 | tf_op jit(solution)/shard_map/ppermute | solution.py:52
  134.1 5.4 %all_to_all.43 = f32[2,1024,128]{2,1,0:T(8,128)} all-to-all(f32[2,1024,128]{2,1,0:T(8,128)S(1)} %reshape.207), channel_id=1, replica_groups=mesh['gx_0'=8,'gx_1'=4,'gx_2'=2,'vert'=8] {'gx_2'}, dimensions={0} | all-to-all | bytes 2097152 | tf_op jit(solution)/shard_map/all_to_all | solution.py:131
  140.8 27.2 %all_to_all.44 = f32[32,32,128]{2,1,0:T(8,128)S(1)} all-to-all(f32[32,32,128]{2,1,0:T(8,128)S(1)} %bitcast.400), channel_id=1, replica_groups=mesh['gx_0'=8,'gx_1'=4,'gx_2'=2,'vert'=8] {'gx_0','gx_1'}, dimensions={0} | all-to-all | bytes 1048576 | tf_op jit(solution)/shard_map/all_to_all | solution.py:131
  168.1 21.4 %all_to_all.45 = f32[32,32,128]{2,1,0:T(8,128)S(1)} all-to-all(f32[32,32,128]{2,1,0:T(8,128)S(1)} %broadcast_in_dim.21), channel_id=1, replica_groups=mesh['gx_0'=8,'gx_1'=4,'gx_2'=2,'vert'=8] {'gx_0','gx_1'}, dimensions={0} | all-to-all | bytes 1048576 | tf_op jit(solution)/shard_map/all_to_all | solution.py:134
  189.6 5.4 %all_to_all.46 = f32[2,1024,128]{2,1,0:T(8,128)} all-to-all(f32[2,1024,128]{2,1,0:T(8,128)S(1)} %broadcast_in_dim.23), channel_id=1, replica_groups=mesh['gx_0'=8,'gx_1'=4,'gx_2'=2,'vert'=8] {'gx_2'}, dimensions={0} | all-to-all | bytes 2097152 | tf_op jit(solution)/shard_map/all_to_all | solution.py:134
  208.2 2.3 copy.101
  220.7 5.6 %collective-permute-start.11 = (f32[1,1,128,256]{3,2,1,0:T(8,128)S(1)}, f32[1,1,128,256]{3,2,1,0:T(8,128)S(1)}, u32[]{:S(2)}, u32[]{:S(2)}) collective-permute-start(f32[1,1,128,256]{3,2,1,0:T(8,128)S(1)} %bitcast.395), channel_id=1, source_target_pairs={{8,0},{16,8},{24,16},{32,24},{40,32},{48,40},{56,48},{64,56},{72,6... | collective-permute-start | bytes 393224 | tf_op jit(solution)/shard_map/ppermute | solution.py:38
  226.4 2.5 collective-permute-start.10
  231.4 4.4 %collective-permute-done.9 = f32[1,1,128,256]{3,2,1,0:T(8,128)S(1)} collective-permute-done((f32[1,1,128,256]{3,2,1,0:T(8,128)S(1)}, f32[1,1,128,256]{3,2,1,0:T(8,128)S(1)}, u32[]{:S(2)}, u32[]{:S(2)}) %collective-permute-start.9) | collective-permute-done | bytes 131104 | tf_op jit(solution)/shard_map/ppermute | solution.py:38
  239.6 5.8 %collective-permute-start.15 = (f32[1,1,128,256]{3,2,1,0:T(8,128)S(1)}, f32[1,1,128,256]{3,2,1,0:T(8,128)S(1)}, u32[]{:S(2)}, u32[]{:S(2)}) collective-permute-start(f32[1,1,128,256]{3,2,1,0:T(8,128)S(1)} %bitcast.408), channel_id=1, source_target_pairs={{8,0},{16,8},{24,16},{32,24},{40,32},{48,40},{56,48},{64,56},{72,6... | collective-permute-start | bytes 393224 | tf_op jit(solution)/shard_map/ppermute | solution.py:38
  246.3 2.2 collective-permute-start.14
  251.1 4.4 %collective-permute-done.13 = f32[1,1,128,256]{3,2,1,0:T(8,128)S(1)} collective-permute-done((f32[1,1,128,256]{3,2,1,0:T(8,128)S(1)}, f32[1,1,128,256]{3,2,1,0:T(8,128)S(1)}, u32[]{:S(2)}, u32[]{:S(2)}) %collective-permute-start.13) | collective-permute-done | bytes 131104 | tf_op jit(solution)/shard_map/ppermute | solution.py:38
  (129 shorter events, 67.7 us)
Async XLA Ops:
  0.6 79.6 %copy-start = (f32[256,256]{1,0:T(8,128)S(1)}, f32[256,256]{1,0:T(8,128)}, u32[]{:S(2)}) copy-start(f32[256,256]{1,0:T(8,128)} %param.5) | copy-start | bytes 786436
  0.6 6.2 %collective-permute-start.3 = (f32[1,1,128,256]{3,2,1,0:T(8,128)}, f32[1,1,128,256]{3,2,1,0:T(8,128)S(1)}, u32[]{:S(2)}, u32[]{:S(2)}) collective-permute-start(f32[1,1,128,256]{3,2,1,0:T(8,128)} %param.6), channel_id=1, source_target_pairs={{8,0},{16,8},{24,16},{32,24},{40,32},{48,40},{56,48},{64,56},{72,6... | collective-permute-start | bytes 393224 | tf_op jit(solution)/shard_map/ppermute | solution.py:52
  4.0 7.1 %collective-permute-start.2 = (f32[1,1,128,256]{3,2,1,0:T(8,128)}, f32[1,1,128,256]{3,2,1,0:T(8,128)S(1)}, u32[]{:S(2)}, u32[]{:S(2)}) collective-permute-start(f32[1,1,128,256]{3,2,1,0:T(8,128)} %param.6), channel_id=1, source_target_pairs={{1,0},{2,1},{3,2},{4,3},{5,4},{6,5},{7,6},{9,8},{10,9},{11,10},{12... | collective-permute-start | bytes 393224 | tf_op jit(solution)/shard_map/ppermute | solution.py:52
  12.4 0.9 copy-start.1
  59.0 21.3 %copy-start.4 = (f32[1,8,16,256]{3,2,1,0:T(8,128)S(1)}, f32[1,8,16,256]{3,2,1,0:T(8,128)}, u32[]{:S(2)}) copy-start(f32[1,8,16,256]{3,2,1,0:T(8,128)} %param.4) | copy-start | bytes 393220
  76.7 17.7 %all-to-all-start.3 = ((f32[8,192,128]{2,1,0:T(8,128)}), f32[8,192,128]{2,1,0:T(8,128)S(1)}, u32[]{:S(2)}, u32[]{:S(2)}) async-start(f32[8,192,128]{2,1,0:T(8,128)} %broadcast_in_dim.18), calls=%async_computation.3 | async-start | bytes 1572864 | tf_op jit(solution)/shard_map/all_to_all | solution.py:134
  80.6 8.5 %collective-permute-start.1 = (f32[1,8,16,256]{3,2,1,0:T(8,128)S(1)}, f32[1,8,16,256]{3,2,1,0:T(8,128)S(1)}, u32[]{:S(2)}, u32[]{:S(2)}) collective-permute-start(f32[1,8,16,256]{3,2,1,0:T(8,128)S(1)} %bitcast.390), channel_id=1, source_target_pairs={{0,8},{8,16},{16,24},{24,32},{32,40},{40,48},{48,56},{56,64},{64,7... | collective-permute-start | bytes 393224 | tf_op jit(solution)/shard_map/ppermute | solution.py:21
  82.9 8.2 %collective-permute-start = (f32[1,8,16,256]{3,2,1,0:T(8,128)S(1)}, f32[1,8,16,256]{3,2,1,0:T(8,128)S(1)}, u32[]{:S(2)}, u32[]{:S(2)}) collective-permute-start(f32[1,8,16,256]{3,2,1,0:T(8,128)S(1)} %bitcast.391), channel_id=1, source_target_pairs={{8,0},{16,8},{24,16},{32,24},{40,32},{48,40},{56,48},{64,56},{72,6... | collective-permute-start | bytes 393224 | tf_op jit(solution)/shard_map/ppermute | solution.py:24
  95.8 1.3 copy-start.5
  98.2 8.4 %collective-permute-start.5 = (f32[1,8,16,256]{3,2,1,0:T(8,128)S(1)}, f32[1,8,16,256]{3,2,1,0:T(8,128)S(1)}, u32[]{:S(2)}, u32[]{:S(2)}) collective-permute-start(f32[1,8,16,256]{3,2,1,0:T(8,128)S(1)} %bitcast.401), channel_id=1, source_target_pairs={{0,8},{8,16},{16,24},{24,32},{32,40},{40,48},{48,56},{56,64},{64,7... | collective-permute-start | bytes 393224 | tf_op jit(solution)/shard_map/ppermute | solution.py:21
  100.1 8.3 %collective-permute-start.4 = (f32[1,8,16,256]{3,2,1,0:T(8,128)S(1)}, f32[1,8,16,256]{3,2,1,0:T(8,128)S(1)}, u32[]{:S(2)}, u32[]{:S(2)}) collective-permute-start(f32[1,8,16,256]{3,2,1,0:T(8,128)S(1)} %bitcast.402), channel_id=1, source_target_pairs={{8,0},{16,8},{24,16},{32,24},{40,32},{48,40},{56,48},{64,56},{72,6... | collective-permute-start | bytes 393224 | tf_op jit(solution)/shard_map/ppermute | solution.py:24
  109.0 8.5 %collective-permute-start.7 = (f32[1,8,16,256]{3,2,1,0:T(8,128)S(1)}, f32[1,8,16,256]{3,2,1,0:T(8,128)S(1)}, u32[]{:S(2)}, u32[]{:S(2)}) collective-permute-start(f32[1,8,16,256]{3,2,1,0:T(8,128)S(1)} %bitcast.404), channel_id=1, source_target_pairs={{0,8},{8,16},{16,24},{24,32},{32,40},{40,48},{48,56},{56,64},{64,7... | collective-permute-start | bytes 393224 | tf_op jit(solution)/shard_map/ppermute | solution.py:21
  110.9 8.4 %collective-permute-start.6 = (f32[1,8,16,256]{3,2,1,0:T(8,128)S(1)}, f32[1,8,16,256]{3,2,1,0:T(8,128)S(1)}, u32[]{:S(2)}, u32[]{:S(2)}) collective-permute-start(f32[1,8,16,256]{3,2,1,0:T(8,128)S(1)} %bitcast.405), channel_id=1, source_target_pairs={{8,0},{16,8},{24,16},{32,24},{40,32},{48,40},{56,48},{64,56},{72,6... | collective-permute-start | bytes 393224 | tf_op jit(solution)/shard_map/ppermute | solution.py:24
  119.9 9.6 %copy-start.2 = (f32[8,16,256]{2,1,0:T(8,128)}, f32[8,16,256]{2,1,0:T(8,128)S(1)}, u32[]{:S(2)}) copy-start(f32[8,16,256]{2,1,0:T(8,128)S(1)} %fusion.36) | copy-start | bytes 393220
  120.3 8.4 %collective-permute-start.8 = (f32[1,8,16,256]{3,2,1,0:T(8,128)S(1)}, f32[1,8,16,256]{3,2,1,0:T(8,128)S(1)}, u32[]{:S(2)}, u32[]{:S(2)}) collective-permute-start(f32[1,8,16,256]{3,2,1,0:T(8,128)S(1)} %bitcast.412), channel_id=1, source_target_pairs={{8,0},{16,8},{24,16},{32,24},{40,32},{48,40},{56,48},{64,56},{72,6... | collective-permute-start | bytes 393224 | tf_op jit(solution)/shard_map/ppermute | solution.py:52
  218.7 11.6 %collective-permute-start.12 = (f32[1,1,128,256]{3,2,1,0:T(8,128)S(1)}, f32[1,1,128,256]{3,2,1,0:T(8,128)S(1)}, u32[]{:S(2)}, u32[]{:S(2)}) collective-permute-start(f32[1,1,128,256]{3,2,1,0:T(8,128)S(1)} %bitcast.394), channel_id=1, source_target_pairs={{0,8},{8,16},{16,24},{24,32},{32,40},{40,48},{48,56},{56,64},{64,7... | collective-permute-start | bytes 393224 | tf_op jit(solution)/shard_map/ppermute | solution.py:37
  220.7 9.6 %collective-permute-start.11 = (f32[1,1,128,256]{3,2,1,0:T(8,128)S(1)}, f32[1,1,128,256]{3,2,1,0:T(8,128)S(1)}, u32[]{:S(2)}, u32[]{:S(2)}) collective-permute-start(f32[1,1,128,256]{3,2,1,0:T(8,128)S(1)} %bitcast.395), channel_id=1, source_target_pairs={{8,0},{16,8},{24,16},{32,24},{40,32},{48,40},{56,48},{64,56},{72,6... | collective-permute-start | bytes 393224 | tf_op jit(solution)/shard_map/ppermute | solution.py:38
  226.4 5.1 %collective-permute-start.10 = (f32[1,1,128,256]{3,2,1,0:T(8,128)S(1)}, f32[1,1,128,256]{3,2,1,0:T(8,128)S(1)}, u32[]{:S(2)}, u32[]{:S(2)}) collective-permute-start(f32[1,1,128,256]{3,2,1,0:T(8,128)S(1)} %bitcast.396), channel_id=1, source_target_pairs={{0,1},{1,2},{2,3},{3,4},{4,5},{5,6},{6,7},{8,9},{9,10},{10,11},{11... | collective-permute-start | bytes 393224 | tf_op jit(solution)/shard_map/ppermute | solution.py:37
  228.9 6.9 %collective-permute-start.9 = (f32[1,1,128,256]{3,2,1,0:T(8,128)S(1)}, f32[1,1,128,256]{3,2,1,0:T(8,128)S(1)}, u32[]{:S(2)}, u32[]{:S(2)}) collective-permute-start(f32[1,1,128,256]{3,2,1,0:T(8,128)S(1)} %bitcast.397), channel_id=1, source_target_pairs={{1,0},{2,1},{3,2},{4,3},{5,4},{6,5},{7,6},{9,8},{10,9},{11,10},{12... | collective-permute-start | bytes 393224 | tf_op jit(solution)/shard_map/ppermute | solution.py:38
  230.3 15.1 %copy-start.3 = (f32[8,16,256]{2,1,0:T(8,128)S(1)}, f32[8,16,256]{2,1,0:T(8,128)}, u32[]{:S(2)}) copy-start(f32[8,16,256]{2,1,0:T(8,128)} %copy-done.2) | copy-start | bytes 393220
  237.7 12.2 %collective-permute-start.16 = (f32[1,1,128,256]{3,2,1,0:T(8,128)S(1)}, f32[1,1,128,256]{3,2,1,0:T(8,128)S(1)}, u32[]{:S(2)}, u32[]{:S(2)}) collective-permute-start(f32[1,1,128,256]{3,2,1,0:T(8,128)S(1)} %bitcast.407), channel_id=1, source_target_pairs={{0,8},{8,16},{16,24},{24,32},{32,40},{40,48},{48,56},{56,64},{64,7... | collective-permute-start | bytes 393224 | tf_op jit(solution)/shard_map/ppermute | solution.py:37
  239.6 10.3 %collective-permute-start.15 = (f32[1,1,128,256]{3,2,1,0:T(8,128)S(1)}, f32[1,1,128,256]{3,2,1,0:T(8,128)S(1)}, u32[]{:S(2)}, u32[]{:S(2)}) collective-permute-start(f32[1,1,128,256]{3,2,1,0:T(8,128)S(1)} %bitcast.408), channel_id=1, source_target_pairs={{8,0},{16,8},{24,16},{32,24},{40,32},{48,40},{56,48},{64,56},{72,6... | collective-permute-start | bytes 393224 | tf_op jit(solution)/shard_map/ppermute | solution.py:38
  246.3 4.7 %collective-permute-start.14 = (f32[1,1,128,256]{3,2,1,0:T(8,128)S(1)}, f32[1,1,128,256]{3,2,1,0:T(8,128)S(1)}, u32[]{:S(2)}, u32[]{:S(2)}) collective-permute-start(f32[1,1,128,256]{3,2,1,0:T(8,128)S(1)} %bitcast.409), channel_id=1, source_target_pairs={{0,1},{1,2},{2,3},{3,4},{4,5},{5,6},{6,7},{8,9},{9,10},{10,11},{11... | collective-permute-start | bytes 393224 | tf_op jit(solution)/shard_map/ppermute | solution.py:37
  248.6 6.9 %collective-permute-start.13 = (f32[1,1,128,256]{3,2,1,0:T(8,128)S(1)}, f32[1,1,128,256]{3,2,1,0:T(8,128)S(1)}, u32[]{:S(2)}, u32[]{:S(2)}) collective-permute-start(f32[1,1,128,256]{3,2,1,0:T(8,128)S(1)} %bitcast.410), channel_id=1, source_target_pairs={{1,0},{2,1},{3,2},{4,3},{5,4},{6,5},{7,6},{9,8},{10,9},{11,10},{12... | collective-permute-start | bytes 393224 | tf_op jit(solution)/shard_map/ppermute | solution.py:38
